TPU v7x, 256 devices: a whole 4x4x8 slice. The times are simulated.
256 devices in a mesh: leaf: 64 (over y, z, core), layer: 4 (over x).
Axes of the slice: x: 4, y: 4, z: 8, core: 2. Of those that a mesh axis runs over, the one named last changes fastest.
Arguments:
- schur_blocks: float32 [64, 2048, 2048], P('leaf', 'layer'), as said below
Outputs:
- merged: float32 [64, 1536, 3072], P('leaf', 'layer')
- cousin_sum: float32 [64, 512, 512], P('leaf', 'layer')
Inputs may be any that keep to these rules, and one draw needn't show every extreme that they name: `schur_blocks`: symmetric and positive definite.
All inputs are finite; a program needn't handle non-finite values.
Results may differ from a plain program's by a relative error of at most 0.0001.
Values sent between devices are 32-bit elements; how exact they have to be, the bound alone decides.
No kernel may reach another device: no remote copies, remote signals or barrier semaphores. Data moves between devices by JAX's collectives and lax.ppermute only.
A program may use at most 64 MiB of HBM per device.

v0:
```python
import jax
import jax.numpy as jnp
from jax import lax
from jax.experimental import pallas as pl
from jax.experimental.pallas import tpu as pltpu
from jax.sharding import PartitionSpec as P

SEP = 512
SHARED = 512
BLOCK = 128
HIGHEST = lax.Precision.HIGHEST


def partner(value, axis, stride):
    mask = 2**stride
    pairs = [(source, source ^ mask) for source in range(lax.axis_size(axis))]
    return lax.ppermute(value, axis, pairs)


def gather_layer(value):
    layers = lax.axis_size("layer")
    pieces = [value]
    for shift in range(1, layers):
        pairs = [((dest + shift) % layers, dest) for dest in range(layers)]
        pieces.append(lax.ppermute(value, "layer", pairs))
    return jnp.concatenate(pieces, axis=0)


def _inv_factor_kernel(a_ref, x_ref, s_ref, w_ref):
    n = a_ref.shape[0]
    s_ref[...] = a_ref[...]
    rows_i = lax.broadcasted_iota(jnp.int32, (n, n), 0)
    cols_i = lax.broadcasted_iota(jnp.int32, (n, n), 1)
    w_ref[...] = jnp.where(rows_i == cols_i, 1.0, 0.0).astype(jnp.float32)
    x_ref[...] = jnp.zeros((n, n), jnp.float32)
    lane = lax.broadcasted_iota(jnp.int32, (1, n), 1)
    for grp in range(n // 8):
        r0 = grp * 8
        span = n - r0
        row_id = lax.broadcasted_iota(jnp.int32, (span, 1), 0) + r0

        def step(i, carry, r0=r0, span=span, row_id=row_id):
            j = r0 + i
            row_j = s_ref[pl.ds(j, 1), :]
            d = jnp.sum(jnp.where(lane == j, row_j, 0.0), axis=1, keepdims=True)
            scale = 1.0 / jnp.sqrt(d)
            l_row = jnp.where(lane >= j, row_j * scale, 0.0)
            x_row = w_ref[pl.ds(j, 1), :] * scale
            x_ref[pl.ds(j, 1), :] = x_row
            rows = s_ref[r0:, :]
            col = jnp.sum(jnp.where(lane == j, rows, 0.0), axis=1, keepdims=True)
            l_col = jnp.where(row_id > j, col * scale, 0.0)
            s_ref[r0:, :] = rows - l_col * l_row
            w_ref[r0:, :] = w_ref[r0:, :] - l_col * x_row
            return carry

        lax.fori_loop(0, 8, step, 0)


def inverse_factor(a):
    n = a.shape[0]
    return pl.pallas_call(
        _inv_factor_kernel,
        out_shape=jax.ShapeDtypeStruct((n, n), jnp.float32),
        in_specs=[pl.BlockSpec(memory_space=pltpu.VMEM)],
        out_specs=pl.BlockSpec(memory_space=pltpu.VMEM),
        scratch_shapes=[pltpu.VMEM((n, n), jnp.float32), pltpu.VMEM((n, n), jnp.float32)],
    )(a)


def mm(a, b):
    return jnp.dot(a, b, precision=HIGHEST, preferred_element_type=jnp.float32)


def mm_nt(a, b):
    return lax.dot_general(
        a, b, (((1,), (1,)), ((), ())), precision=HIGHEST, preferred_element_type=jnp.float32
    )


def blocked_cholesky(sepmat):
    n = sepmat.shape[0]
    nb = n // BLOCK
    trailing = sepmat
    panels = []
    inverses = []
    for k in range(nb):
        diag = trailing[:BLOCK, :BLOCK]
        inv = inverse_factor(diag)
        inverses.append(inv)
        if k + 1 < nb:
            below = trailing[BLOCK:, :BLOCK]
            panel = mm_nt(below, inv)
            panels.append(panel)
            trailing = trailing[BLOCK:, BLOCK:] - mm_nt(panel, panel)
    return panels, inverses


def forward_solve(panels, inverses, rhs):
    nb = len(inverses)
    out = []
    rest = rhs
    for k in range(nb):
        gk = mm(inverses[k], rest[:BLOCK])
        out.append(gk)
        if k + 1 < nb:
            rest = rest[BLOCK:] - mm(panels[k], gk)
    return jnp.concatenate(out, axis=0)


def on_device(schur_blocks):
    layers = lax.axis_size("layer")
    local = schur_blocks[0]
    slab = local.shape[0]
    sep_slab = SEP // layers
    outer_slab = slab - sep_slab
    shared_slab = SHARED // layers
    outer_all = local.shape[1] - SEP
    me = lax.axis_index("layer")
    parity = lax.axis_index("leaf") % 2

    sep_rows = local[:sep_slab]
    sep_cols = jnp.concatenate(
        [sep_rows[:, h * slab : h * slab + sep_slab] for h in range(layers)], axis=1
    )
    out_cols = jnp.concatenate(
        [sep_rows[:, h * slab + sep_slab : (h + 1) * slab] for h in range(layers)], axis=1
    )
    sibling = partner(sep_cols, "leaf", 0)
    rows_rel = gather_layer(sep_cols + sibling)
    doubled = jnp.concatenate([rows_rel, rows_rel], axis=1)
    sepmat = lax.dynamic_slice_in_dim(doubled, me * sep_slab, SEP, axis=1)

    out_cols, sepmat = lax.optimization_barrier((out_cols, sepmat))
    coupling_own = gather_layer(out_cols)
    coupling_sib = partner(coupling_own, "leaf", 0)

    panels, inverses = blocked_cholesky(sepmat)
    joined = forward_solve(panels, inverses, jnp.concatenate([coupling_own, coupling_sib], axis=1))
    factor_own = lax.dynamic_slice_in_dim(joined, me * outer_slab, outer_slab, axis=1)

    direct_rows = jnp.concatenate(
        [local[sep_slab:, h * slab + sep_slab : (h + 1) * slab] for h in range(layers)], axis=1
    )
    product = lax.dot_general(
        factor_own, joined, (((0,), (0,)), ((), ())), precision=HIGHEST,
        preferred_element_type=jnp.float32,
    )
    with_own = direct_rows - product[:, :outer_all]
    with_sib = -product[:, outer_all:]
    merged = jnp.where(
        parity == 0,
        jnp.concatenate([with_own, with_sib], axis=1),
        jnp.concatenate([with_sib, with_own], axis=1),
    )
    own_shared = jnp.concatenate(
        [with_own[:shared_slab, h * outer_slab : h * outer_slab + shared_slab] for h in range(layers)],
        axis=1,
    )
    cousin = partner(own_shared, "leaf", 1)
    cousin_sum = own_shared + cousin
    return (merged[None], cousin_sum[None])


def solution(mesh):
    placed = (P("leaf", "layer", None),)
    return jax.shard_map(
        on_device,
        mesh=mesh,
        in_specs=placed,
        out_specs=(P("leaf", "layer", None), P("leaf", "layer", None)),
        check_vma=False,
    )
```

profile of v0, /device:TPU:1, one launch (start us, length us, event | category | flops | bytes accessed | tf_op | source)
XLA Modules:
  0.0 173.1 jit_solution(15785435925025926205)
XLA Ops:
  0.6 1.3 slice_bitcast_fusion
  2.0 3.3 %collective-permute-start = (f32[128,512]{1,0:T(8,128)S(1)}, f32[128,512]{1,0:T(8,128)S(1)}, u32[]{:S(2)}, u32[]{:S(2)}) collective-permute-start(f32[128,512]{1,0:T(8,128)S(1)} %pad_maximum_fusion.3), channel_id=1, source_target_pairs={{0,4},{4,0},{8,12},{12,8},{16,20},{20,16},{24,28},{28,24},{32,36},... | collective-permute-start | bytes 786440 | tf_op jit(solution)/shard_map/ppermute | solution.py:17
  5.3 1.2 collective-permute-done
  8.6 5.4 %collective-permute-done.1 = f32[128,512]{1,0:T(8,128)S(1)} collective-permute-done((f32[128,512]{1,0:T(8,128)S(1)}, f32[128,512]{1,0:T(8,128)S(1)}, u32[]{:S(2)}, u32[]{:S(2)}) %collective-permute-start.1) | collective-permute-done | bytes 262176 | tf_op jit(solution)/shard_map/ppermute | solution.py:25
  14.1 2.0 %collective-permute-done.2 = f32[128,512]{1,0:T(8,128)S(1)} collective-permute-done((f32[128,512]{1,0:T(8,128)S(1)}, f32[128,512]{1,0:T(8,128)S(1)}, u32[]{:S(2)}, u32[]{:S(2)}) %collective-permute-start.2) | collective-permute-done | bytes 262176 | tf_op jit(solution)/shard_map/ppermute | solution.py:25
  16.1 6.6 %collective-permute-done.3 = f32[128,512]{1,0:T(8,128)S(1)} collective-permute-done((f32[128,512]{1,0:T(8,128)S(1)}, f32[128,512]{1,0:T(8,128)S(1)}, u32[]{:S(2)}, u32[]{:S(2)}) %collective-permute-start.3) | collective-permute-done | bytes 262176 | tf_op jit(solution)/shard_map/ppermute | solution.py:25
  22.7 1.5 fusion.14
  25.8 17.1 %collective-permute-done.4 = f32[128,1536]{1,0:T(8,128)S(1)} collective-permute-done((f32[128,1536]{1,0:T(8,128)S(1)}, f32[128,1536]{1,0:T(8,128)S(1)}, u32[]{:S(2)}, u32[]{:S(2)}) %collective-permute-start.4) | collective-permute-done | bytes 786464 | tf_op jit(solution)/shard_map/ppermute | solution.py:25
  43.8 18.2 %collective-permute-done.6 = f32[128,1536]{1,0:T(8,128)S(1)} collective-permute-done((f32[128,1536]{1,0:T(8,128)S(1)}, f32[128,1536]{1,0:T(8,128)S(1)}, u32[]{:S(2)}, u32[]{:S(2)}) %collective-permute-start.6) | collective-permute-done | bytes 786464 | tf_op jit(solution)/shard_map/ppermute | solution.py:25
  62.9 3.1 %fusion.29 = (f32[384,384]{1,0:T(8,128)}, f32[384,384]{1,0:T(8,128)}, f32[384,384]{1,0:T(8,128)}, f32[384,384]{1,0:T(8,128)}) fusion(f32[512,2048]{1,0:T(8,128)} %bitcast.29), kind=kLoop, calls=%fused_computation.56 | loop fusion | bytes 4718592 | tf_op jit(solution)/shard_map/slice | solution.py:143
  66.0 1.5 slice.119.a_ref
  67.4 14.9 %shard_map.30 = f32[128,128]{1,0:T(8,128)} custom-call(f32[128,128]{1,0:T(8,128)} %slice.119.a_ref), custom_call_target="tpu_custom_call" | custom-call | tf_op jit(solution)/shard_map/pallas_call | solution.py:62
  82.4 1.3 fusion.20
  83.7 1.7 convolution_subtract_fusion
  86.8 14.9 %shard_map.31 = f32[128,128]{1,0:T(8,128)} custom-call(f32[128,128]{1,0:T(8,128)} %slice.152.a_ref), custom_call_target="tpu_custom_call" | custom-call | tf_op jit(solution)/shard_map/pallas_call | solution.py:62
  101.8 1.2 fusion.22
  103.0 1.3 convolution_subtract_fusion.1
  105.7 14.9 %shard_map.32 = f32[128,128]{1,0:T(8,128)} custom-call(f32[128,128]{1,0:T(8,128)} %slice.156.a_ref), custom_call_target="tpu_custom_call" | custom-call | tf_op jit(solution)/shard_map/pallas_call | solution.py:62
  120.6 1.1 fusion.24
  121.7 1.7 %convolution_subtract_fusion.2.a_ref = f32[128,128]{1,0:T(8,128)} fusion(f32[128,128]{1,0:T(8,128)S(1)} %fusion.24, f32[256,256]{1,0:T(8,128)} %copy-done.5), kind=kOutput, calls=%fused_computation.28 | convolution fusion | flops 25182208 | bytes 262144 | tf_op jit(solution)/shard_map/dot_general | solution.py:76
  123.5 14.9 %shard_map.33 = f32[128,128]{1,0:T(8,128)} custom-call(f32[128,128]{1,0:T(8,128)} %convolution_subtract_fusion.2.a_ref), custom_call_target="tpu_custom_call" | custom-call | tf_op jit(solution)/shard_map/pallas_call | solution.py:62
  138.4 2.6 %fusion.7 = f32[128,3072]{1,0:T(8,128)S(1)} fusion(f32[128,128]{1,0:T(8,128)} %shard_map.30, f32[512,1536]{1,0:T(8,128)} %collective-permute-done.7, f32[512,1536]{1,0:T(8,128)S(1)} %constant_dynamic-update-slice_fusion), kind=kOutput, calls=%fused_computation.22 | convolution fusion | flops 604372992 | bytes 7929856 | tf_op jit(solution)/shard_map/dot_general | solution.py:72
  141.0 4.8 %fusion = f32[384,3072]{1,0:T(8,128)S(1)} fusion(f32[512,1536]{1,0:T(8,128)} %collective-permute-done.7, f32[512,1536]{1,0:T(8,128)S(1)} %constant_dynamic-update-slice_fusion, f32[384,128]{1,0:T(8,128)S(1)} %fusion.20, f32[128,3072]{1,0:T(8,128)S(1)} %fusion.7), kind=kOutput, calls=%fused_computation.2 | convolution fusion | flops 1814298624 | bytes 12779520 | tf_op jit(solution)/shard_map/dot_general | solution.py:72
  145.8 1.5 fusion.5
  147.3 2.8 %slice_subtract_fusion = f32[256,3072]{1,0:T(8,128)S(1)} fusion(f32[384,3072]{1,0:T(8,128)S(1)} %fusion, f32[256,128]{1,0:T(8,128)S(1)} %fusion.22, f32[128,3072]{1,0:T(8,128)S(1)} %fusion.5), kind=kOutput, calls=%fused_computation.4 | convolution fusion | flops 1208745984 | bytes 7995392 | tf_op jit(solution)/shard_map/dot_general | solution.py:72
  150.1 1.5 fusion.3
  151.6 1.5 fusion.33
  153.1 1.4 fusion.2
  155.3 8.1 %fusion.18 = f32[384,3072]{1,0:T(8,128)S(1)} fusion(f32[512,3072]{1,0:T(8,128)S(1)} %pad_maximum_fusion, s32[]{:T(128)S(6)} %select_n.31), kind=kOutput, calls=%fused_computation.38 | convolution fusion | flops 7247757312 | bytes 11796484 | tf_op jit(solution)/shard_map/dot_general | solution.py:145
  164.1 1.7 collective-permute-start.8
  165.8 2.9 %maximum_select_fusion = f32[1,384,3072]{2,1,0:T(8,128)} fusion(f32[1,384,1536]{2,1,0:T(8,128)S(1)} %get-tuple-element.7, f32[1,384,1536]{2,1,0:T(8,128)S(1)} %bitcast.28, pred[]{:T(512)S(6)} %eq.5), kind=kLoop, calls=%fused_computation.3 | loop fusion | flops 3538944 | bytes 9437185 | tf_op jit(solution)/shard_map/jit(_where)/select_n | solution.py:151
  168.7 3.6 %collective-permute-done.8 = f32[128,512]{1,0:T(8,128)S(1)} collective-permute-done((f32[128,512]{1,0:T(8,128)S(1)}, f32[128,512]{1,0:T(8,128)S(1)}, u32[]{:S(2)}, u32[]{:S(2)}) %collective-permute-start.8) | collective-permute-done | bytes 262176 | tf_op jit(solution)/shard_map/ppermute | solution.py:17
  (43 shorter events, 10.4 us)
Async XLA Ops:
  2.0 4.5 %collective-permute-start = (f32[128,512]{1,0:T(8,128)S(1)}, f32[128,512]{1,0:T(8,128)S(1)}, u32[]{:S(2)}, u32[]{:S(2)}) collective-permute-start(f32[128,512]{1,0:T(8,128)S(1)} %pad_maximum_fusion.3), channel_id=1, source_target_pairs={{0,4},{4,0},{8,12},{12,8},{16,20},{20,16},{24,28},{28,24},{32,36},... | collective-permute-start | bytes 786440 | tf_op jit(solution)/shard_map/ppermute | solution.py:17
  6.5 7.6 %collective-permute-start.1 = (f32[128,512]{1,0:T(8,128)S(1)}, f32[128,512]{1,0:T(8,128)S(1)}, u32[]{:S(2)}, u32[]{:S(2)}) collective-permute-start(f32[128,512]{1,0:T(8,128)S(1)} %fusion.28), channel_id=1, source_target_pairs={{1,0},{2,1},{3,2},{0,3},{5,4},{6,5},{7,6},{4,7},{9,8},{10,9},{11,1... | collective-permute-start | bytes 786440 | tf_op jit(solution)/shard_map/ppermute | solution.py:25
  7.4 8.8 %collective-permute-start.2 = (f32[128,512]{1,0:T(8,128)S(1)}, f32[128,512]{1,0:T(8,128)S(1)}, u32[]{:S(2)}, u32[]{:S(2)}) collective-permute-start(f32[128,512]{1,0:T(8,128)S(1)} %fusion.28), channel_id=1, source_target_pairs={{2,0},{3,1},{0,2},{1,3},{6,4},{7,5},{4,6},{5,7},{10,8},{11,9},{8,1... | collective-permute-start | bytes 786440 | tf_op jit(solution)/shard_map/ppermute | solution.py:25
  7.9 14.8 %collective-permute-start.3 = (f32[128,512]{1,0:T(8,128)S(1)}, f32[128,512]{1,0:T(8,128)S(1)}, u32[]{:S(2)}, u32[]{:S(2)}) collective-permute-start(f32[128,512]{1,0:T(8,128)S(1)} %fusion.28), channel_id=1, source_target_pairs={{3,0},{0,1},{1,2},{2,3},{7,4},{4,5},{5,6},{6,7},{11,8},{8,9},{9,10... | collective-permute-start | bytes 786440 | tf_op jit(solution)/shard_map/ppermute | solution.py:25
  24.2 18.6 %collective-permute-start.4 = (f32[128,1536]{1,0:T(8,128)S(1)}, f32[128,1536]{1,0:T(8,128)S(1)}, u32[]{:S(2)}, u32[]{:S(2)}) collective-permute-start(f32[128,1536]{1,0:T(8,128)S(1)} %pad_maximum_fusion.2), channel_id=1, source_target_pairs={{1,0},{2,1},{3,2},{0,3},{5,4},{6,5},{7,6},{4,7},{9,8},{10,9},{11,1... | collective-permute-start | bytes 2359304 | tf_op jit(solution)/shard_map/ppermute | solution.py:25
  24.2 19.6 %collective-permute-start.5 = (f32[128,1536]{1,0:T(8,128)S(1)}, f32[128,1536]{1,0:T(8,128)S(1)}, u32[]{:S(2)}, u32[]{:S(2)}) collective-permute-start(f32[128,1536]{1,0:T(8,128)S(1)} %pad_maximum_fusion.2), channel_id=1, source_target_pairs={{2,0},{3,1},{0,2},{1,3},{6,4},{7,5},{4,6},{5,7},{10,8},{11,9},{8,1... | collective-permute-start | bytes 2359304 | tf_op jit(solution)/shard_map/ppermute | solution.py:25
  24.8 37.3 %collective-permute-start.6 = (f32[128,1536]{1,0:T(8,128)S(1)}, f32[128,1536]{1,0:T(8,128)S(1)}, u32[]{:S(2)}, u32[]{:S(2)}) collective-permute-start(f32[128,1536]{1,0:T(8,128)S(1)} %pad_maximum_fusion.2), channel_id=1, source_target_pairs={{3,0},{0,1},{1,2},{2,3},{7,4},{4,5},{5,6},{6,7},{11,8},{8,9},{9,10... | collective-permute-start | bytes 2359304 | tf_op jit(solution)/shard_map/ppermute | solution.py:25
  62.1 76.3 %collective-permute-start.7 = (f32[512,1536]{1,0:T(8,128)S(1)}, f32[512,1536]{1,0:T(8,128)}, u32[]{:S(2)}, u32[]{:S(2)}) collective-permute-start(f32[512,1536]{1,0:T(8,128)S(1)} %constant_dynamic-update-slice_fusion), channel_id=1, source_target_pairs={{0,4},{4,0},{8,12},{12,8},{16,20},{20,16},{24,28},{28,24},{32,36},... | collective-permute-start | bytes 9437192 | tf_op jit(solution)/shard_map/ppermute | solution.py:17
  85.4 0.8 copy-start.4
  104.3 0.7 copy-start.5
  141.0 4.8 %copy-start.6 = (f32[128,128]{1,0:T(8,128)S(1)}, f32[128,128]{1,0:T(8,128)}, u32[]{:S(2)}) copy-start(f32[128,128]{1,0:T(8,128)} %shard_map.31) | copy-start | bytes 196612
  147.3 2.8 %copy-start.7 = (f32[128,128]{1,0:T(8,128)S(1)}, f32[128,128]{1,0:T(8,128)}, u32[]{:S(2)}) copy-start(f32[128,128]{1,0:T(8,128)} %shard_map.32) | copy-start | bytes 196612
  150.1 3.0 %copy-start.8 = (f32[128,128]{1,0:T(8,128)S(1)}, f32[128,128]{1,0:T(8,128)}, u32[]{:S(2)}) copy-start(f32[128,128]{1,0:T(8,128)} %shard_map.33) | copy-start | bytes 196612
  155.2 8.2 %copy-start = (f32[384,384]{1,0:T(8,128)S(1)}, f32[384,384]{1,0:T(8,128)}, u32[]{:S(2)}) copy-start(f32[384,384]{1,0:T(8,128)} %get-tuple-element.8) | copy-start | bytes 1769476
  155.2 8.2 %copy-start.1 = (f32[384,384]{1,0:T(8,128)S(1)}, f32[384,384]{1,0:T(8,128)}, u32[]{:S(2)}) copy-start(f32[384,384]{1,0:T(8,128)} %get-tuple-element.9) | copy-start | bytes 1769476
  155.3 8.2 %copy-start.2 = (f32[384,384]{1,0:T(8,128)S(1)}, f32[384,384]{1,0:T(8,128)}, u32[]{:S(2)}) copy-start(f32[384,384]{1,0:T(8,128)} %get-tuple-element.10) | copy-start | bytes 1769476
  155.3 8.2 %copy-start.3 = (f32[384,384]{1,0:T(8,128)S(1)}, f32[384,384]{1,0:T(8,128)}, u32[]{:S(2)}) copy-start(f32[384,384]{1,0:T(8,128)} %get-tuple-element.11) | copy-start | bytes 1769476
  164.1 8.3 %collective-permute-start.8 = (f32[128,512]{1,0:T(8,128)S(1)}, f32[128,512]{1,0:T(8,128)S(1)}, u32[]{:S(2)}, u32[]{:S(2)}) collective-permute-start(f32[128,512]{1,0:T(8,128)S(1)} %pad_maximum_fusion.4), channel_id=1, source_target_pairs={{0,8},{4,12},{8,0},{12,4},{16,24},{20,28},{24,16},{28,20},{32,40},... | collective-permute-start | bytes 786440 | tf_op jit(solution)/shard_map/ppermute | solution.py:17
where the time goes:
time: 174 us; the launch traced here: 173 us
  Pallas kernels  59.8 us (34%)
  waiting for transfers between devices  55 us (32%)
  matrix products  32.5 us (19%)
  starting transfers between devices  9.21 us (5%)
  local copies, waits for them, and re-layouts  9.02 us (5%)
  other arithmetic  6.63 us (4%)
    pallas_call x4, Pallas kernels, inverse_factor(): pl.pallas_call(_inv_factor_kernel, out_shape=jax.ShapeDtypeStruct((n, n),...  59.8 us
    ppermute x6, waiting for transfers between devices, gather_layer(): pieces.append(lax.ppermute(value, 'layer', pairs))  50.2 us
    dot_general x7, matrix products, mm(): return jnp.dot(a, b, precision=HIGHEST, preferred_element_type=jnp.float32)  16 us
    dot_general x6, matrix products, mm_nt(): lax.dot_general(a, b, (((1,), (1,)), ((), ())), precision=HIGHEST, prefer...  8.37 us
    dot_general x1, matrix products, on_device(): lax.dot_general(factor_own, joined, (((0,), (0,)), ((), ())), precision=H...  8.12 us
    ppermute x3, starting transfers between devices, partner(): return lax.ppermute(value, axis, pairs)  5.77 us
    ppermute x3, waiting for transfers between devices, partner(): return lax.ppermute(value, axis, pairs)  4.78 us
  transfers between devices with their start and end apart: 9, of which 8 were waited for; matrix products, arithmetic and copies ran while one was open for 10% of the time, Pallas kernels for 35%

commit v1 on v0

--- a/solution.py
+++ b/solution.py
@@ -4,6 +4,7 @@
 from jax.experimental import pallas as pl
 from jax.experimental.pallas import tpu as pltpu
 from jax.sharding import PartitionSpec as P
+
 
 SEP = 512
 SHARED = 512
@@ -108,7 +109,7 @@
     return jnp.concatenate(out, axis=0)
 
 
-def on_device(schur_blocks):
+def condense(schur_blocks):
     layers = lax.axis_size("layer")
     local = schur_blocks[0]
     slab = local.shape[0]
@@ -142,6 +143,14 @@
     direct_rows = jnp.concatenate(
         [local[sep_slab:, h * slab + sep_slab : (h + 1) * slab] for h in range(layers)], axis=1
     )
+    shared_of = lambda m: jnp.concatenate(
+        [m[:, h * outer_slab : h * outer_slab + shared_slab] for h in range(layers)], axis=1
+    )
+    own_shared = shared_of(direct_rows[:shared_slab]) - lax.dot_general(
+        factor_own[:, :shared_slab], shared_of(joined[:, :outer_all]), (((0,), (0,)), ((), ())),
+        precision=HIGHEST, preferred_element_type=jnp.float32,
+    )
+    cousin = partner(own_shared, "leaf", 1)
     product = lax.dot_general(
         factor_own, joined, (((0,), (0,)), ((), ())), precision=HIGHEST,
         preferred_element_type=jnp.float32,
@@ -153,11 +162,6 @@
         jnp.concatenate([with_own, with_sib], axis=1),
         jnp.concatenate([with_sib, with_own], axis=1),
     )
-    own_shared = jnp.concatenate(
-        [with_own[:shared_slab, h * outer_slab : h * outer_slab + shared_slab] for h in range(layers)],
-        axis=1,
-    )
-    cousin = partner(own_shared, "leaf", 1)
     cousin_sum = own_shared + cousin
     return (merged[None], cousin_sum[None])
 
@@ -165,7 +169,7 @@
 def solution(mesh):
     placed = (P("leaf", "layer", None),)
     return jax.shard_map(
-        on_device,
+        condense,
         mesh=mesh,
         in_specs=placed,
         out_specs=(P("leaf", "layer", None), P("leaf", "layer", None)),

time: 174 us -> 176 us (1.011)
    slice x5 -> x6, local copies, waits for them, and re-layouts: 4.54 us -> 6.2 us  [the longest x1 3.06 us: condense(): local[sep_slab:, h * slab + sep_slab:(h + 1) * slab]]
    dot_general x1 -> x2, matrix products: 8.12 us -> 8.97 us  [the longest x1 8.16 us: condense(): lax.dot_general(factor_own, joined, (((0,), (0,)), ((), ())), precision=H...]
  transfers between devices with their start and end apart: 9 -> 9, of which waited for: 8 -> 8; matrix products, arithmetic and copies ran while one was open for 10% -> 11% of each run, Pallas kernels for 35% -> 34%
where the time goes in v1:
time: 176 us; the launch traced here: 175 us
  Pallas kernels  59.7 us (34%)
  waiting for transfers between devices  54.4 us (31%)
  matrix products  33.3 us (19%)
  local copies, waits for them, and re-layouts  10.7 us (6%)
  starting transfers between devices  9.22 us (5%)
  other arithmetic  6.97 us (4%)
    pallas_call x4, Pallas kernels, inverse_factor(): pl.pallas_call(_inv_factor_kernel, out_shape=jax.ShapeDtypeStruct((n, n),...  59.7 us
    ppermute x6, waiting for transfers between devices, gather_layer(): pieces.append(lax.ppermute(value, 'layer', pairs))  50.2 us
    dot_general x7, matrix products, mm(): return jnp.dot(a, b, precision=HIGHEST, preferred_element_type=jnp.float32)  16 us
    dot_general x6, matrix products, mm_nt(): lax.dot_general(a, b, (((1,), (1,)), ((), ())), precision=HIGHEST, prefer...  8.36 us
    dot_general x1, matrix products, condense(): lax.dot_general(factor_own, joined, (((0,), (0,)), ((), ())), precision=H...  8.16 us
    ppermute x3, starting transfers between devices, partner(): return lax.ppermute(value, axis, pairs)  5.78 us
    ppermute x3, waiting for transfers between devices, partner(): return lax.ppermute(value, axis, pairs)  4.15 us
  transfers between devices with their start and end apart: 9, of which 8 were waited for; matrix products, arithmetic and copies ran while one was open for 11% of the time, Pallas kernels for 34%

profile of v1, /device:TPU:1, one launch (start us, length us, event | category | flops | bytes accessed | tf_op | source)
XLA Modules:
  0.0 175.3 jit_solution(3842600544604985216)
XLA Ops:
  0.6 1.3 slice_bitcast_fusion
  2.0 3.3 %collective-permute-start = (f32[128,512]{1,0:T(8,128)S(1)}, f32[128,512]{1,0:T(8,128)S(1)}, u32[]{:S(2)}, u32[]{:S(2)}) collective-permute-start(f32[128,512]{1,0:T(8,128)S(1)} %pad_maximum_fusion.3), channel_id=1, source_target_pairs={{0,4},{4,0},{8,12},{12,8},{16,20},{20,16},{24,28},{28,24},{32,36},... | collective-permute-start | bytes 786440 | tf_op jit(solution)/shard_map/ppermute | solution.py:18
  5.3 1.2 collective-permute-done
  8.6 5.4 %collective-permute-done.1 = f32[128,512]{1,0:T(8,128)S(1)} collective-permute-done((f32[128,512]{1,0:T(8,128)S(1)}, f32[128,512]{1,0:T(8,128)S(1)}, u32[]{:S(2)}, u32[]{:S(2)}) %collective-permute-start.1) | collective-permute-done | bytes 262176 | tf_op jit(solution)/shard_map/ppermute | solution.py:26
  14.1 2.0 %collective-permute-done.2 = f32[128,512]{1,0:T(8,128)S(1)} collective-permute-done((f32[128,512]{1,0:T(8,128)S(1)}, f32[128,512]{1,0:T(8,128)S(1)}, u32[]{:S(2)}, u32[]{:S(2)}) %collective-permute-start.2) | collective-permute-done | bytes 262176 | tf_op jit(solution)/shard_map/ppermute | solution.py:26
  16.1 6.6 %collective-permute-done.3 = f32[128,512]{1,0:T(8,128)S(1)} collective-permute-done((f32[128,512]{1,0:T(8,128)S(1)}, f32[128,512]{1,0:T(8,128)S(1)}, u32[]{:S(2)}, u32[]{:S(2)}) %collective-permute-start.3) | collective-permute-done | bytes 262176 | tf_op jit(solution)/shard_map/ppermute | solution.py:26
  22.7 1.5 fusion.15
  25.8 17.1 %collective-permute-done.4 = f32[128,1536]{1,0:T(8,128)S(1)} collective-permute-done((f32[128,1536]{1,0:T(8,128)S(1)}, f32[128,1536]{1,0:T(8,128)S(1)}, u32[]{:S(2)}, u32[]{:S(2)}) %collective-permute-start.4) | collective-permute-done | bytes 786464 | tf_op jit(solution)/shard_map/ppermute | solution.py:26
  43.8 18.2 %collective-permute-done.6 = f32[128,1536]{1,0:T(8,128)S(1)} collective-permute-done((f32[128,1536]{1,0:T(8,128)S(1)}, f32[128,1536]{1,0:T(8,128)S(1)}, u32[]{:S(2)}, u32[]{:S(2)}) %collective-permute-start.6) | collective-permute-done | bytes 786464 | tf_op jit(solution)/shard_map/ppermute | solution.py:26
  62.9 1.6 fusion.41
  64.5 3.1 %fusion.42 = (f32[384,384]{1,0:T(8,128)}, f32[384,384]{1,0:T(8,128)}, f32[384,384]{1,0:T(8,128)}, f32[384,384]{1,0:T(8,128)}) fusion(f32[512,2048]{1,0:T(8,128)} %bitcast.30), kind=kLoop, calls=%fused_computation.69 | loop fusion | bytes 4718592 | tf_op jit(solution)/shard_map/slice | solution.py:144
  67.6 1.5 slice.152.a_ref
  69.1 14.9 %shard_map.30 = f32[128,128]{1,0:T(8,128)} custom-call(f32[128,128]{1,0:T(8,128)} %slice.152.a_ref), custom_call_target="tpu_custom_call" | custom-call | tf_op jit(solution)/shard_map/pallas_call | solution.py:63
  84.0 1.3 fusion.29
  85.3 1.7 convolution_subtract_fusion
  88.4 14.9 %shard_map.31 = f32[128,128]{1,0:T(8,128)} custom-call(f32[128,128]{1,0:T(8,128)} %slice.190.a_ref), custom_call_target="tpu_custom_call" | custom-call | tf_op jit(solution)/shard_map/pallas_call | solution.py:63
  103.4 1.2 fusion.31
  104.5 1.3 convolution_subtract_fusion.1
  107.2 14.9 %shard_map.32 = f32[128,128]{1,0:T(8,128)} custom-call(f32[128,128]{1,0:T(8,128)} %slice.194.a_ref), custom_call_target="tpu_custom_call" | custom-call | tf_op jit(solution)/shard_map/pallas_call | solution.py:63
  123.3 1.7 convolution_subtract_fusion.3.a_ref
  125.0 14.9 %shard_map.33 = f32[128,128]{1,0:T(8,128)} custom-call(f32[128,128]{1,0:T(8,128)} %convolution_subtract_fusion.3.a_ref), custom_call_target="tpu_custom_call" | custom-call | tf_op jit(solution)/shard_map/pallas_call | solution.py:63
  140.0 2.6 %fusion.8 = f32[128,3072]{1,0:T(8,128)S(1)} fusion(f32[128,128]{1,0:T(8,128)} %shard_map.30, f32[512,1536]{1,0:T(8,128)} %collective-permute-done.7, f32[512,1536]{1,0:T(8,128)S(1)} %constant_dynamic-update-slice_fusion), kind=kOutput, calls=%fused_computation.23 | convolution fusion | flops 604372992 | bytes 7929856 | tf_op jit(solution)/shard_map/dot_general | solution.py:73
  142.6 4.8 %fusion = f32[384,3072]{1,0:T(8,128)S(1)} fusion(f32[512,1536]{1,0:T(8,128)} %collective-permute-done.7, f32[512,1536]{1,0:T(8,128)S(1)} %constant_dynamic-update-slice_fusion, f32[384,128]{1,0:T(8,128)S(1)} %fusion.29, f32[128,3072]{1,0:T(8,128)S(1)} %fusion.8), kind=kOutput, calls=%fused_computation.2 | convolution fusion | flops 1814298624 | bytes 12779520 | tf_op jit(solution)/shard_map/dot_general | solution.py:73
  147.4 1.5 fusion.6
  148.9 2.8 %slice_subtract_fusion = f32[256,3072]{1,0:T(8,128)S(1)} fusion(f32[384,3072]{1,0:T(8,128)S(1)} %fusion, f32[256,128]{1,0:T(8,128)S(1)} %fusion.31, f32[128,3072]{1,0:T(8,128)S(1)} %fusion.6), kind=kOutput, calls=%fused_computation.4 | convolution fusion | flops 1208745984 | bytes 7995392 | tf_op jit(solution)/shard_map/dot_general | solution.py:73
  151.7 1.5 fusion.4
  153.1 1.5 fusion.45
  154.6 1.4 fusion.3
  157.3 8.2 %fusion.26 = f32[384,3072]{1,0:T(8,128)S(1)} fusion(f32[512,3072]{1,0:T(8,128)S(1)} %pad_maximum_fusion, s32[]{:T(128)S(6)} %select_n.31), kind=kOutput, calls=%fused_computation.47 | convolution fusion | flops 7247757312 | bytes 11796484 | tf_op jit(solution)/shard_map/dot_general | solution.py:154
  166.3 1.7 collective-permute-start.8
  168.7 2.9 %maximum_select_fusion = f32[1,384,3072]{2,1,0:T(8,128)} fusion(f32[1,384,1536]{2,1,0:T(8,128)S(1)} %get-tuple-element.11, f32[1,384,1536]{2,1,0:T(8,128)S(1)} %get-tuple-element.10, pred[]{:T(512)S(6)} %eq.5), kind=kLoop, calls=%fused_computation.3 | loop fusion | flops 3538944 | bytes 9437185 | tf_op jit(solution)/shard_map/jit(_where)/select_n | solution.py:160
  171.6 3.0 %collective-permute-done.8 = f32[128,512]{1,0:T(8,128)S(1)} collective-permute-done((f32[128,512]{1,0:T(8,128)S(1)}, f32[128,512]{1,0:T(8,128)S(1)}, u32[]{:S(2)}, u32[]{:S(2)}) %collective-permute-start.8) | collective-permute-done | bytes 262176 | tf_op jit(solution)/shard_map/ppermute | solution.py:18
  (52 shorter events, 12.8 us)
Async XLA Ops:
  2.0 4.5 %collective-permute-start = (f32[128,512]{1,0:T(8,128)S(1)}, f32[128,512]{1,0:T(8,128)S(1)}, u32[]{:S(2)}, u32[]{:S(2)}) collective-permute-start(f32[128,512]{1,0:T(8,128)S(1)} %pad_maximum_fusion.3), channel_id=1, source_target_pairs={{0,4},{4,0},{8,12},{12,8},{16,20},{20,16},{24,28},{28,24},{32,36},... | collective-permute-start | bytes 786440 | tf_op jit(solution)/shard_map/ppermute | solution.py:18
  6.5 7.6 %collective-permute-start.1 = (f32[128,512]{1,0:T(8,128)S(1)}, f32[128,512]{1,0:T(8,128)S(1)}, u32[]{:S(2)}, u32[]{:S(2)}) collective-permute-start(f32[128,512]{1,0:T(8,128)S(1)} %fusion.39), channel_id=1, source_target_pairs={{1,0},{2,1},{3,2},{0,3},{5,4},{6,5},{7,6},{4,7},{9,8},{10,9},{11,1... | collective-permute-start | bytes 786440 | tf_op jit(solution)/shard_map/ppermute | solution.py:26
  7.4 8.8 %collective-permute-start.2 = (f32[128,512]{1,0:T(8,128)S(1)}, f32[128,512]{1,0:T(8,128)S(1)}, u32[]{:S(2)}, u32[]{:S(2)}) collective-permute-start(f32[128,512]{1,0:T(8,128)S(1)} %fusion.39), channel_id=1, source_target_pairs={{2,0},{3,1},{0,2},{1,3},{6,4},{7,5},{4,6},{5,7},{10,8},{11,9},{8,1... | collective-permute-start | bytes 786440 | tf_op jit(solution)/shard_map/ppermute | solution.py:26
  7.9 14.8 %collective-permute-start.3 = (f32[128,512]{1,0:T(8,128)S(1)}, f32[128,512]{1,0:T(8,128)S(1)}, u32[]{:S(2)}, u32[]{:S(2)}) collective-permute-start(f32[128,512]{1,0:T(8,128)S(1)} %fusion.39), channel_id=1, source_target_pairs={{3,0},{0,1},{1,2},{2,3},{7,4},{4,5},{5,6},{6,7},{11,8},{8,9},{9,10... | collective-permute-start | bytes 786440 | tf_op jit(solution)/shard_map/ppermute | solution.py:26
  24.2 18.6 %collective-permute-start.4 = (f32[128,1536]{1,0:T(8,128)S(1)}, f32[128,1536]{1,0:T(8,128)S(1)}, u32[]{:S(2)}, u32[]{:S(2)}) collective-permute-start(f32[128,1536]{1,0:T(8,128)S(1)} %pad_maximum_fusion.2), channel_id=1, source_target_pairs={{1,0},{2,1},{3,2},{0,3},{5,4},{6,5},{7,6},{4,7},{9,8},{10,9},{11,1... | collective-permute-start | bytes 2359304 | tf_op jit(solution)/shard_map/ppermute | solution.py:26
  24.2 19.6 %collective-permute-start.5 = (f32[128,1536]{1,0:T(8,128)S(1)}, f32[128,1536]{1,0:T(8,128)S(1)}, u32[]{:S(2)}, u32[]{:S(2)}) collective-permute-start(f32[128,1536]{1,0:T(8,128)S(1)} %pad_maximum_fusion.2), channel_id=1, source_target_pairs={{2,0},{3,1},{0,2},{1,3},{6,4},{7,5},{4,6},{5,7},{10,8},{11,9},{8,1... | collective-permute-start | bytes 2359304 | tf_op jit(solution)/shard_map/ppermute | solution.py:26
  24.8 37.3 %collective-permute-start.6 = (f32[128,1536]{1,0:T(8,128)S(1)}, f32[128,1536]{1,0:T(8,128)S(1)}, u32[]{:S(2)}, u32[]{:S(2)}) collective-permute-start(f32[128,1536]{1,0:T(8,128)S(1)} %pad_maximum_fusion.2), channel_id=1, source_target_pairs={{3,0},{0,1},{1,2},{2,3},{7,4},{4,5},{5,6},{6,7},{11,8},{8,9},{9,10... | collective-permute-start | bytes 2359304 | tf_op jit(solution)/shard_map/ppermute | solution.py:26
  62.1 77.9 %collective-permute-start.7 = (f32[512,1536]{1,0:T(8,128)S(1)}, f32[512,1536]{1,0:T(8,128)}, u32[]{:S(2)}, u32[]{:S(2)}) collective-permute-start(f32[512,1536]{1,0:T(8,128)S(1)} %constant_dynamic-update-slice_fusion), channel_id=1, source_target_pairs={{0,4},{4,0},{8,12},{12,8},{16,20},{20,16},{24,28},{28,24},{32,36},... | collective-permute-start | bytes 9437192 | tf_op jit(solution)/shard_map/ppermute | solution.py:18
  87.0 0.8 copy-start.4
  105.9 0.7 copy-start.5
  142.6 4.8 %copy-start.6 = (f32[128,128]{1,0:T(8,128)S(1)}, f32[128,128]{1,0:T(8,128)}, u32[]{:S(2)}) copy-start(f32[128,128]{1,0:T(8,128)} %shard_map.31) | copy-start | bytes 196612
  148.8 2.8 %copy-start.7 = (f32[128,128]{1,0:T(8,128)S(1)}, f32[128,128]{1,0:T(8,128)}, u32[]{:S(2)}) copy-start(f32[128,128]{1,0:T(8,128)} %shard_map.32) | copy-start | bytes 196612
  151.7 3.0 %copy-start.8 = (f32[128,128]{1,0:T(8,128)S(1)}, f32[128,128]{1,0:T(8,128)}, u32[]{:S(2)}) copy-start(f32[128,128]{1,0:T(8,128)} %shard_map.33) | copy-start | bytes 196612
  157.2 8.2 %copy-start.9 = (f32[128,128]{1,0:T(8,128)S(1)}, f32[128,128]{1,0:T(8,128)}, u32[]{:S(2)}) copy-start(f32[128,128]{1,0:T(8,128)} %get-tuple-element.12) | copy-start | bytes 196612
  157.2 8.2 %copy-start.10 = (f32[128,128]{1,0:T(8,128)S(1)}, f32[128,128]{1,0:T(8,128)}, u32[]{:S(2)}) copy-start(f32[128,128]{1,0:T(8,128)} %get-tuple-element.13) | copy-start | bytes 196612
  157.2 8.2 %copy-start.11 = (f32[128,128]{1,0:T(8,128)S(1)}, f32[128,128]{1,0:T(8,128)}, u32[]{:S(2)}) copy-start(f32[128,128]{1,0:T(8,128)} %get-tuple-element.14) | copy-start | bytes 196612
  157.2 8.2 %copy-start.12 = (f32[128,128]{1,0:T(8,128)S(1)}, f32[128,128]{1,0:T(8,128)}, u32[]{:S(2)}) copy-start(f32[128,128]{1,0:T(8,128)} %get-tuple-element.15) | copy-start | bytes 196612
  157.2 10.8 %copy-start = (f32[384,384]{1,0:T(8,128)S(1)}, f32[384,384]{1,0:T(8,128)}, u32[]{:S(2)}) copy-start(f32[384,384]{1,0:T(8,128)} %get-tuple-element.16) | copy-start | bytes 1769476
  157.2 10.8 %copy-start.1 = (f32[384,384]{1,0:T(8,128)S(1)}, f32[384,384]{1,0:T(8,128)}, u32[]{:S(2)}) copy-start(f32[384,384]{1,0:T(8,128)} %get-tuple-element.17) | copy-start | bytes 1769476
  157.3 10.8 %copy-start.2 = (f32[384,384]{1,0:T(8,128)S(1)}, f32[384,384]{1,0:T(8,128)}, u32[]{:S(2)}) copy-start(f32[384,384]{1,0:T(8,128)} %get-tuple-element.18) | copy-start | bytes 1769476
  157.3 10.8 %copy-start.3 = (f32[384,384]{1,0:T(8,128)S(1)}, f32[384,384]{1,0:T(8,128)}, u32[]{:S(2)}) copy-start(f32[384,384]{1,0:T(8,128)} %get-tuple-element.19) | copy-start | bytes 1769476
  166.3 8.3 %collective-permute-start.8 = (f32[128,512]{1,0:T(8,128)S(1)}, f32[128,512]{1,0:T(8,128)S(1)}, u32[]{:S(2)}, u32[]{:S(2)}) collective-permute-start(f32[128,512]{1,0:T(8,128)S(1)} %convolution_subtract_fusion.2), channel_id=1, source_target_pairs={{0,8},{4,12},{8,0},{12,4},{16,24},{20,28},{24,16},{28,20},{32,40},... | collective-permute-start | bytes 786440 | tf_op jit(solution)/shard_map/ppermute | solution.py:18

commit v2 on v1

--- a/solution.py
+++ b/solution.py
@@ -79,14 +79,14 @@
     )
 
 
-def blocked_cholesky(sepmat):
+def blocked_cholesky(sepmat, first_diag):
     n = sepmat.shape[0]
     nb = n // BLOCK
     trailing = sepmat
     panels = []
     inverses = []
     for k in range(nb):
-        diag = trailing[:BLOCK, :BLOCK]
+        diag = first_diag if k == 0 else trailing[:BLOCK, :BLOCK]
         inv = inverse_factor(diag)
         inverses.append(inv)
         if k + 1 < nb:
@@ -128,7 +128,9 @@
         [sep_rows[:, h * slab + sep_slab : (h + 1) * slab] for h in range(layers)], axis=1
     )
     sibling = partner(sep_cols, "leaf", 0)
-    rows_rel = gather_layer(sep_cols + sibling)
+    summed = sep_cols + sibling
+    first_diag = lax.dynamic_slice_in_dim(summed, me * sep_slab, sep_slab, axis=1)
+    rows_rel = gather_layer(summed)
     doubled = jnp.concatenate([rows_rel, rows_rel], axis=1)
     sepmat = lax.dynamic_slice_in_dim(doubled, me * sep_slab, SEP, axis=1)
 
@@ -136,7 +138,7 @@
     coupling_own = gather_layer(out_cols)
     coupling_sib = partner(coupling_own, "leaf", 0)
 
-    panels, inverses = blocked_cholesky(sepmat)
+    panels, inverses = blocked_cholesky(sepmat, first_diag)
     joined = forward_solve(panels, inverses, jnp.concatenate([coupling_own, coupling_sib], axis=1))
     factor_own = lax.dynamic_slice_in_dim(joined, me * outer_slab, outer_slab, axis=1)
 

time: 176 us -> 175 us (level)
  no operation moved by 1% of the time
where the time goes in v2:
time: 175 us; the launch traced here: 174 us
  Pallas kernels  59.7 us (34%)
  waiting for transfers between devices  54.4 us (31%)
  matrix products  33.3 us (19%)
  local copies, waits for them, and re-layouts  9.87 us (6%)
  starting transfers between devices  9.22 us (5%)
  other arithmetic  6.86 us (4%)
    pallas_call x4, Pallas kernels, inverse_factor(): pl.pallas_call(_inv_factor_kernel, out_shape=jax.ShapeDtypeStruct((n, n),...  59.7 us
    ppermute x6, waiting for transfers between devices, gather_layer(): pieces.append(lax.ppermute(value, 'layer', pairs))  50.2 us
    dot_general x7, matrix products, mm(): return jnp.dot(a, b, precision=HIGHEST, preferred_element_type=jnp.float32)  16 us
    dot_general x6, matrix products, mm_nt(): lax.dot_general(a, b, (((1,), (1,)), ((), ())), precision=HIGHEST, prefer...  8.36 us
    dot_general x1, matrix products, condense(): lax.dot_general(factor_own, joined, (((0,), (0,)), ((), ())), precision=H...  8.16 us
    ppermute x3, starting transfers between devices, partner(): return lax.ppermute(value, axis, pairs)  5.78 us
    ppermute x3, waiting for transfers between devices, partner(): return lax.ppermute(value, axis, pairs)  4.15 us
  transfers between devices with their start and end apart: 9, of which 8 were waited for; matrix products, arithmetic and copies ran while one was open for 11% of the time, Pallas kernels for 34%

profile of v2, /device:TPU:1, one launch (start us, length us, event | category | flops | bytes accessed | tf_op | source)
XLA Modules:
  0.0 174.4 jit_solution(7326821714062618188)
XLA Ops:
  0.6 1.3 slice_bitcast_fusion
  2.0 3.3 %collective-permute-start = (f32[128,512]{1,0:T(8,128)S(1)}, f32[128,512]{1,0:T(8,128)S(1)}, u32[]{:S(2)}, u32[]{:S(2)}) collective-permute-start(f32[128,512]{1,0:T(8,128)S(1)} %pad_maximum_fusion.3), channel_id=1, source_target_pairs={{0,4},{4,0},{8,12},{12,8},{16,20},{20,16},{24,28},{28,24},{32,36},... | collective-permute-start | bytes 786440 | tf_op jit(solution)/shard_map/ppermute | solution.py:18
  5.3 1.2 collective-permute-done
  8.6 5.4 %collective-permute-done.1 = f32[128,512]{1,0:T(8,128)S(1)} collective-permute-done((f32[128,512]{1,0:T(8,128)S(1)}, f32[128,512]{1,0:T(8,128)S(1)}, u32[]{:S(2)}, u32[]{:S(2)}) %collective-permute-start.1) | collective-permute-done | bytes 262176 | tf_op jit(solution)/shard_map/ppermute | solution.py:26
  14.1 2.0 %collective-permute-done.2 = f32[128,512]{1,0:T(8,128)S(1)} collective-permute-done((f32[128,512]{1,0:T(8,128)S(1)}, f32[128,512]{1,0:T(8,128)S(1)}, u32[]{:S(2)}, u32[]{:S(2)}) %collective-permute-start.2) | collective-permute-done | bytes 262176 | tf_op jit(solution)/shard_map/ppermute | solution.py:26
  16.1 6.6 %collective-permute-done.3 = f32[128,512]{1,0:T(8,128)S(1)} collective-permute-done((f32[128,512]{1,0:T(8,128)S(1)}, f32[128,512]{1,0:T(8,128)S(1)}, u32[]{:S(2)}, u32[]{:S(2)}) %collective-permute-start.3) | collective-permute-done | bytes 262176 | tf_op jit(solution)/shard_map/ppermute | solution.py:26
  22.7 1.5 fusion.15
  25.8 17.1 %collective-permute-done.4 = f32[128,1536]{1,0:T(8,128)S(1)} collective-permute-done((f32[128,1536]{1,0:T(8,128)S(1)}, f32[128,1536]{1,0:T(8,128)S(1)}, u32[]{:S(2)}, u32[]{:S(2)}) %collective-permute-start.4) | collective-permute-done | bytes 786464 | tf_op jit(solution)/shard_map/ppermute | solution.py:26
  43.8 18.2 %collective-permute-done.6 = f32[128,1536]{1,0:T(8,128)S(1)} collective-permute-done((f32[128,1536]{1,0:T(8,128)S(1)}, f32[128,1536]{1,0:T(8,128)S(1)}, u32[]{:S(2)}, u32[]{:S(2)}) %collective-permute-start.6) | collective-permute-done | bytes 786464 | tf_op jit(solution)/shard_map/ppermute | solution.py:26
  62.9 1.6 fusion.41
  64.5 3.1 %fusion.42 = (f32[384,384]{1,0:T(8,128)}, f32[384,384]{1,0:T(8,128)}, f32[384,384]{1,0:T(8,128)}, f32[384,384]{1,0:T(8,128)}) fusion(f32[512,2048]{1,0:T(8,128)} %bitcast.30), kind=kLoop, calls=%fused_computation.70 | loop fusion | bytes 4718592 | tf_op jit(solution)/shard_map/slice | solution.py:146
  68.2 14.9 %shard_map.30 = f32[128,128]{1,0:T(8,128)} custom-call(f32[128,128]{1,0:T(8,128)} %constant_dynamic-slice_fusion.a_ref), custom_call_target="tpu_custom_call" | custom-call | tf_op jit(solution)/shard_map/pallas_call | solution.py:63
  83.2 1.3 fusion.29
  84.4 1.7 convolution_subtract_fusion
  87.6 14.9 %shard_map.31 = f32[128,128]{1,0:T(8,128)} custom-call(f32[128,128]{1,0:T(8,128)} %slice.186.a_ref), custom_call_target="tpu_custom_call" | custom-call | tf_op jit(solution)/shard_map/pallas_call | solution.py:63
  102.5 1.2 fusion.31
  103.7 1.3 convolution_subtract_fusion.1
  106.4 14.9 %shard_map.32 = f32[128,128]{1,0:T(8,128)} custom-call(f32[128,128]{1,0:T(8,128)} %slice.190.a_ref), custom_call_target="tpu_custom_call" | custom-call | tf_op jit(solution)/shard_map/pallas_call | solution.py:63
  121.3 1.1 fusion.33
  122.5 1.7 convolution_subtract_fusion.3.a_ref
  124.2 14.9 %shard_map.33 = f32[128,128]{1,0:T(8,128)} custom-call(f32[128,128]{1,0:T(8,128)} %convolution_subtract_fusion.3.a_ref), custom_call_target="tpu_custom_call" | custom-call | tf_op jit(solution)/shard_map/pallas_call | solution.py:63
  139.1 2.6 %fusion.8 = f32[128,3072]{1,0:T(8,128)S(1)} fusion(f32[128,128]{1,0:T(8,128)} %shard_map.30, f32[512,1536]{1,0:T(8,128)} %collective-permute-done.7, f32[512,1536]{1,0:T(8,128)S(1)} %constant_dynamic-update-slice_fusion), kind=kOutput, calls=%fused_computation.23 | convolution fusion | flops 604372992 | bytes 7929856 | tf_op jit(solution)/shard_map/dot_general | solution.py:73
  141.8 4.8 %fusion = f32[384,3072]{1,0:T(8,128)S(1)} fusion(f32[512,1536]{1,0:T(8,128)} %collective-permute-done.7, f32[512,1536]{1,0:T(8,128)S(1)} %constant_dynamic-update-slice_fusion, f32[384,128]{1,0:T(8,128)S(1)} %fusion.29, f32[128,3072]{1,0:T(8,128)S(1)} %fusion.8), kind=kOutput, calls=%fused_computation.2 | convolution fusion | flops 1814298624 | bytes 12779520 | tf_op jit(solution)/shard_map/dot_general | solution.py:73
  146.5 1.5 fusion.6
  148.0 2.8 %slice_subtract_fusion = f32[256,3072]{1,0:T(8,128)S(1)} fusion(f32[384,3072]{1,0:T(8,128)S(1)} %fusion, f32[256,128]{1,0:T(8,128)S(1)} %fusion.31, f32[128,3072]{1,0:T(8,128)S(1)} %fusion.6), kind=kOutput, calls=%fused_computation.4 | convolution fusion | flops 1208745984 | bytes 7995392 | tf_op jit(solution)/shard_map/dot_general | solution.py:73
  150.8 1.5 fusion.4
  152.3 1.5 fusion.45
  153.8 1.4 fusion.3
  156.3 8.2 %fusion.26 = f32[384,3072]{1,0:T(8,128)S(1)} fusion(f32[512,3072]{1,0:T(8,128)S(1)} %pad_maximum_fusion, s32[]{:T(128)S(6)} %select_n.35), kind=kOutput, calls=%fused_computation.47 | convolution fusion | flops 7247757312 | bytes 11796484 | tf_op jit(solution)/shard_map/dot_general | solution.py:156
  165.4 1.7 collective-permute-start.8
  167.7 2.9 %maximum_select_fusion = f32[1,384,3072]{2,1,0:T(8,128)} fusion(f32[1,384,1536]{2,1,0:T(8,128)S(1)} %get-tuple-element.11, f32[1,384,1536]{2,1,0:T(8,128)S(1)} %get-tuple-element.10, pred[]{:T(512)S(6)} %eq.5), kind=kLoop, calls=%fused_computation.3 | loop fusion | flops 3538944 | bytes 9437185 | tf_op jit(solution)/shard_map/jit(_where)/select_n | solution.py:162
  170.7 3.0 %collective-permute-done.8 = f32[128,512]{1,0:T(8,128)S(1)} collective-permute-done((f32[128,512]{1,0:T(8,128)S(1)}, f32[128,512]{1,0:T(8,128)S(1)}, u32[]{:S(2)}, u32[]{:S(2)}) %collective-permute-start.8) | collective-permute-done | bytes 262176 | tf_op jit(solution)/shard_map/ppermute | solution.py:18
  (52 shorter events, 12.2 us)
Async XLA Ops:
  2.0 4.5 %collective-permute-start = (f32[128,512]{1,0:T(8,128)S(1)}, f32[128,512]{1,0:T(8,128)S(1)}, u32[]{:S(2)}, u32[]{:S(2)}) collective-permute-start(f32[128,512]{1,0:T(8,128)S(1)} %pad_maximum_fusion.3), channel_id=1, source_target_pairs={{0,4},{4,0},{8,12},{12,8},{16,20},{20,16},{24,28},{28,24},{32,36},... | collective-permute-start | bytes 786440 | tf_op jit(solution)/shard_map/ppermute | solution.py:18
  6.5 7.6 %collective-permute-start.1 = (f32[128,512]{1,0:T(8,128)S(1)}, f32[128,512]{1,0:T(8,128)S(1)}, u32[]{:S(2)}, u32[]{:S(2)}) collective-permute-start(f32[128,512]{1,0:T(8,128)S(1)} %fusion.39), channel_id=1, source_target_pairs={{1,0},{2,1},{3,2},{0,3},{5,4},{6,5},{7,6},{4,7},{9,8},{10,9},{11,1... | collective-permute-start | bytes 786440 | tf_op jit(solution)/shard_map/ppermute | solution.py:26
  7.4 8.8 %collective-permute-start.2 = (f32[128,512]{1,0:T(8,128)S(1)}, f32[128,512]{1,0:T(8,128)S(1)}, u32[]{:S(2)}, u32[]{:S(2)}) collective-permute-start(f32[128,512]{1,0:T(8,128)S(1)} %fusion.39), channel_id=1, source_target_pairs={{2,0},{3,1},{0,2},{1,3},{6,4},{7,5},{4,6},{5,7},{10,8},{11,9},{8,1... | collective-permute-start | bytes 786440 | tf_op jit(solution)/shard_map/ppermute | solution.py:26
  7.9 14.8 %collective-permute-start.3 = (f32[128,512]{1,0:T(8,128)S(1)}, f32[128,512]{1,0:T(8,128)S(1)}, u32[]{:S(2)}, u32[]{:S(2)}) collective-permute-start(f32[128,512]{1,0:T(8,128)S(1)} %fusion.39), channel_id=1, source_target_pairs={{3,0},{0,1},{1,2},{2,3},{7,4},{4,5},{5,6},{6,7},{11,8},{8,9},{9,10... | collective-permute-start | bytes 786440 | tf_op jit(solution)/shard_map/ppermute | solution.py:26
  24.2 18.6 %collective-permute-start.4 = (f32[128,1536]{1,0:T(8,128)S(1)}, f32[128,1536]{1,0:T(8,128)S(1)}, u32[]{:S(2)}, u32[]{:S(2)}) collective-permute-start(f32[128,1536]{1,0:T(8,128)S(1)} %pad_maximum_fusion.2), channel_id=1, source_target_pairs={{1,0},{2,1},{3,2},{0,3},{5,4},{6,5},{7,6},{4,7},{9,8},{10,9},{11,1... | collective-permute-start | bytes 2359304 | tf_op jit(solution)/shard_map/ppermute | solution.py:26
  24.2 19.6 %collective-permute-start.5 = (f32[128,1536]{1,0:T(8,128)S(1)}, f32[128,1536]{1,0:T(8,128)S(1)}, u32[]{:S(2)}, u32[]{:S(2)}) collective-permute-start(f32[128,1536]{1,0:T(8,128)S(1)} %pad_maximum_fusion.2), channel_id=1, source_target_pairs={{2,0},{3,1},{0,2},{1,3},{6,4},{7,5},{4,6},{5,7},{10,8},{11,9},{8,1... | collective-permute-start | bytes 2359304 | tf_op jit(solution)/shard_map/ppermute | solution.py:26
  24.8 37.3 %collective-permute-start.6 = (f32[128,1536]{1,0:T(8,128)S(1)}, f32[128,1536]{1,0:T(8,128)S(1)}, u32[]{:S(2)}, u32[]{:S(2)}) collective-permute-start(f32[128,1536]{1,0:T(8,128)S(1)} %pad_maximum_fusion.2), channel_id=1, source_target_pairs={{3,0},{0,1},{1,2},{2,3},{7,4},{4,5},{5,6},{6,7},{11,8},{8,9},{9,10... | collective-permute-start | bytes 2359304 | tf_op jit(solution)/shard_map/ppermute | solution.py:26
  62.1 77.0 %collective-permute-start.7 = (f32[512,1536]{1,0:T(8,128)S(1)}, f32[512,1536]{1,0:T(8,128)}, u32[]{:S(2)}, u32[]{:S(2)}) collective-permute-start(f32[512,1536]{1,0:T(8,128)S(1)} %constant_dynamic-update-slice_fusion), channel_id=1, source_target_pairs={{0,4},{4,0},{8,12},{12,8},{16,20},{20,16},{24,28},{28,24},{32,36},... | collective-permute-start | bytes 9437192 | tf_op jit(solution)/shard_map/ppermute | solution.py:18
  86.1 0.8 copy-start.4
  105.1 0.7 copy-start.5
  141.7 4.8 %copy-start.6 = (f32[128,128]{1,0:T(8,128)S(1)}, f32[128,128]{1,0:T(8,128)}, u32[]{:S(2)}) copy-start(f32[128,128]{1,0:T(8,128)} %shard_map.31) | copy-start | bytes 196612
  148.0 2.8 %copy-start.7 = (f32[128,128]{1,0:T(8,128)S(1)}, f32[128,128]{1,0:T(8,128)}, u32[]{:S(2)}) copy-start(f32[128,128]{1,0:T(8,128)} %shard_map.32) | copy-start | bytes 196612
  150.8 3.0 %copy-start.8 = (f32[128,128]{1,0:T(8,128)S(1)}, f32[128,128]{1,0:T(8,128)}, u32[]{:S(2)}) copy-start(f32[128,128]{1,0:T(8,128)} %shard_map.33) | copy-start | bytes 196612
  156.2 8.2 %copy-start.9 = (f32[128,128]{1,0:T(8,128)S(1)}, f32[128,128]{1,0:T(8,128)}, u32[]{:S(2)}) copy-start(f32[128,128]{1,0:T(8,128)} %get-tuple-element.12) | copy-start | bytes 196612
  156.3 8.2 %copy-start.10 = (f32[128,128]{1,0:T(8,128)S(1)}, f32[128,128]{1,0:T(8,128)}, u32[]{:S(2)}) copy-start(f32[128,128]{1,0:T(8,128)} %get-tuple-element.13) | copy-start | bytes 196612
  156.3 8.2 %copy-start.11 = (f32[128,128]{1,0:T(8,128)S(1)}, f32[128,128]{1,0:T(8,128)}, u32[]{:S(2)}) copy-start(f32[128,128]{1,0:T(8,128)} %get-tuple-element.14) | copy-start | bytes 196612
  156.3 8.2 %copy-start.12 = (f32[128,128]{1,0:T(8,128)S(1)}, f32[128,128]{1,0:T(8,128)}, u32[]{:S(2)}) copy-start(f32[128,128]{1,0:T(8,128)} %get-tuple-element.15) | copy-start | bytes 196612
  156.3 10.8 %copy-start = (f32[384,384]{1,0:T(8,128)S(1)}, f32[384,384]{1,0:T(8,128)}, u32[]{:S(2)}) copy-start(f32[384,384]{1,0:T(8,128)} %get-tuple-element.16) | copy-start | bytes 1769476
  156.3 10.8 %copy-start.1 = (f32[384,384]{1,0:T(8,128)S(1)}, f32[384,384]{1,0:T(8,128)}, u32[]{:S(2)}) copy-start(f32[384,384]{1,0:T(8,128)} %get-tuple-element.17) | copy-start | bytes 1769476
  156.3 10.8 %copy-start.2 = (f32[384,384]{1,0:T(8,128)S(1)}, f32[384,384]{1,0:T(8,128)}, u32[]{:S(2)}) copy-start(f32[384,384]{1,0:T(8,128)} %get-tuple-element.18) | copy-start | bytes 1769476
  156.3 10.8 %copy-start.3 = (f32[384,384]{1,0:T(8,128)S(1)}, f32[384,384]{1,0:T(8,128)}, u32[]{:S(2)}) copy-start(f32[384,384]{1,0:T(8,128)} %get-tuple-element.19) | copy-start | bytes 1769476
  165.4 8.3 %collective-permute-start.8 = (f32[128,512]{1,0:T(8,128)S(1)}, f32[128,512]{1,0:T(8,128)S(1)}, u32[]{:S(2)}, u32[]{:S(2)}) collective-permute-start(f32[128,512]{1,0:T(8,128)S(1)} %convolution_subtract_fusion.2), channel_id=1, source_target_pairs={{0,8},{4,12},{8,0},{12,4},{16,24},{20,28},{24,16},{28,20},{32,40},... | collective-permute-start | bytes 786440 | tf_op jit(solution)/shard_map/ppermute | solution.py:18

commit v3 on v2

--- a/solution.py
+++ b/solution.py
@@ -49,8 +49,8 @@
             x_row = w_ref[pl.ds(j, 1), :] * scale
             x_ref[pl.ds(j, 1), :] = x_row
             rows = s_ref[r0:, :]
-            col = jnp.sum(jnp.where(lane == j, rows, 0.0), axis=1, keepdims=True)
-            l_col = jnp.where(row_id > j, col * scale, 0.0)
+            col = jnp.transpose(jnp.broadcast_to(l_row, (n, n)))[r0:, :]
+            l_col = jnp.where(row_id > j, col, 0.0)
             s_ref[r0:, :] = rows - l_col * l_row
             w_ref[r0:, :] = w_ref[r0:, :] - l_col * x_row
             return carry
@@ -116,7 +116,6 @@
     sep_slab = SEP // layers
     outer_slab = slab - sep_slab
     shared_slab = SHARED // layers
-    outer_all = local.shape[1] - SEP
     me = lax.axis_index("layer")
     parity = lax.axis_index("leaf") % 2
 
@@ -136,29 +135,27 @@
 
     out_cols, sepmat = lax.optimization_barrier((out_cols, sepmat))
     coupling_own = gather_layer(out_cols)
-    coupling_sib = partner(coupling_own, "leaf", 0)
 
     panels, inverses = blocked_cholesky(sepmat, first_diag)
-    joined = forward_solve(panels, inverses, jnp.concatenate([coupling_own, coupling_sib], axis=1))
-    factor_own = lax.dynamic_slice_in_dim(joined, me * outer_slab, outer_slab, axis=1)
+    joined_own = forward_solve(panels, inverses, coupling_own)
+    joined_sib = partner(joined_own, "leaf", 0)
+    factor_own = lax.dynamic_slice_in_dim(joined_own, me * outer_slab, outer_slab, axis=1)
 
     direct_rows = jnp.concatenate(
         [local[sep_slab:, h * slab + sep_slab : (h + 1) * slab] for h in range(layers)], axis=1
     )
-    shared_of = lambda m: jnp.concatenate(
-        [m[:, h * outer_slab : h * outer_slab + shared_slab] for h in range(layers)], axis=1
+    contract = (((0,), (0,)), ((), ()))
+    with_own = direct_rows - lax.dot_general(
+        factor_own, joined_own, contract, precision=HIGHEST, preferred_element_type=jnp.float32
     )
-    own_shared = shared_of(direct_rows[:shared_slab]) - lax.dot_general(
-        factor_own[:, :shared_slab], shared_of(joined[:, :outer_all]), (((0,), (0,)), ((), ())),
-        precision=HIGHEST, preferred_element_type=jnp.float32,
+    own_shared = jnp.concatenate(
+        [with_own[:shared_slab, h * outer_slab : h * outer_slab + shared_slab] for h in range(layers)],
+        axis=1,
     )
     cousin = partner(own_shared, "leaf", 1)
-    product = lax.dot_general(
-        factor_own, joined, (((0,), (0,)), ((), ())), precision=HIGHEST,
-        preferred_element_type=jnp.float32,
+    with_sib = -lax.dot_general(
+        factor_own, joined_sib, contract, precision=HIGHEST, preferred_element_type=jnp.float32
     )
-    with_own = direct_rows - product[:, :outer_all]
-    with_sib = -product[:, outer_all:]
     merged = jnp.where(
         parity == 0,
         jnp.concatenate([with_own, with_sib], axis=1),

time: 175 us -> 168 us (0.960)
  Pallas kernels: 59.7 us -> 107 us
  waiting for transfers between devices: 54.4 us -> 9.1 us
  matrix products: 33.3 us -> 24.8 us
  starting transfers between devices: 9.22 us -> 13.1 us
  local copies, waits for them, and re-layouts: 9.87 us -> 6.53 us
    ppermute x6, waiting for transfers between devices: 50.2 us -> 0.02 us  [gather_layer(): pieces.append(lax.ppermute(value, 'layer', pairs))]
    pallas_call x4, Pallas kernels: 59.7 us -> 107 us  [inverse_factor(): pl.pallas_call(_inv_factor_kernel, out_shape=jax.ShapeDtypeStruct((n, n),...]
    dot_general x7, matrix products: 16 us -> 9.37 us  [mm(): return jnp.dot(a, b, precision=HIGHEST, preferred_element_type=jnp.float32)]
    ppermute x3, waiting for transfers between devices: 4.15 us -> 9.08 us  [partner(): return lax.ppermute(value, axis, pairs)]
    ppermute x6, starting transfers between devices: 3.44 us -> 7.27 us  [gather_layer(): pieces.append(lax.ppermute(value, 'layer', pairs))]
    dot_general x6, matrix products: 8.36 us -> 5.32 us  [mm_nt(): lax.dot_general(a, b, (((1,), (1,)), ((), ())), precision=HIGHEST, prefer...]
  transfers between devices with their start and end apart: 9 -> 9, of which waited for: 8 -> 2; matrix products, arithmetic and copies ran while one was open for 11% -> 10% of each run, Pallas kernels for 34% -> 64%
where the time goes in v3:
time: 168 us; the launch traced here: 167 us
  Pallas kernels  107 us (64%)
  matrix products  24.8 us (15%)
  starting transfers between devices  13.1 us (8%)
  waiting for transfers between devices  9.1 us (5%)
  local copies, waits for them, and re-layouts  6.53 us (4%)
  other arithmetic  6.21 us (4%)
    pallas_call x4, Pallas kernels, inverse_factor(): pl.pallas_call(_inv_factor_kernel, out_shape=jax.ShapeDtypeStruct((n, n),...  107 us
    dot_general x7, matrix products, mm(): return jnp.dot(a, b, precision=HIGHEST, preferred_element_type=jnp.float32)  9.37 us
    ppermute x3, waiting for transfers between devices, partner(): return lax.ppermute(value, axis, pairs)  9.08 us
    ppermute x6, starting transfers between devices, gather_layer(): pieces.append(lax.ppermute(value, 'layer', pairs))  7.27 us
    dot_general x1, matrix products, condense(): lax.dot_general(factor_own, joined_sib, contract, precision=HIGHEST, pref...  6.07 us
    ppermute x3, starting transfers between devices, partner(): return lax.ppermute(value, axis, pairs)  5.8 us
    dot_general x6, matrix products, mm_nt(): lax.dot_general(a, b, (((1,), (1,)), ((), ())), precision=HIGHEST, prefer...  5.32 us
    dot_general x1, matrix products, condense(): lax.dot_general(factor_own, joined_own, contract, precision=HIGHEST, pref...  3.99 us
  transfers between devices with their start and end apart: 9, of which 2 were waited for; matrix products, arithmetic and copies ran while one was open for 10% of the time, Pallas kernels for 64%

profile of v3, /device:TPU:1, one launch (start us, length us, event | category | flops | bytes accessed | tf_op | source)
XLA Modules:
  0.0 167.4 jit_solution(15621909270839932140)
XLA Ops:
  0.6 1.3 slice_bitcast_fusion
  2.0 3.3 %collective-permute-start = (f32[128,512]{1,0:T(8,128)S(1)}, f32[128,512]{1,0:T(8,128)S(1)}, u32[]{:S(2)}, u32[]{:S(2)}) collective-permute-start(f32[128,512]{1,0:T(8,128)S(1)} %pad_maximum_fusion.2), channel_id=1, source_target_pairs={{0,4},{4,0},{8,12},{12,8},{16,20},{20,16},{24,28},{28,24},{32,36},... | collective-permute-start | bytes 786440 | tf_op jit(solution)/shard_map/ppermute | solution.py:18
  5.4 1.1 collective-permute-done
  6.5 0.8 collective-permute-start.1
  9.2 26.7 %shard_map.30 = f32[128,128]{1,0:T(8,128)} custom-call(f32[128,128]{1,0:T(8,128)} %constant_dynamic-slice_fusion.a_ref), custom_call_target="tpu_custom_call" | custom-call | tf_op jit(solution)/shard_map/pallas_call | solution.py:63
  36.5 1.6 collective-permute-start.6
  38.1 1.7 %collective-permute-start.5 = (f32[128,1536]{1,0:T(8,128)S(1)}, f32[128,1536]{1,0:T(8,128)S(1)}, u32[]{:S(2)}, u32[]{:S(2)}) collective-permute-start(f32[128,1536]{1,0:T(8,128)S(1)} %pad_maximum_fusion.1), channel_id=1, source_target_pairs={{2,0},{3,1},{0,2},{1,3},{6,4},{7,5},{4,6},{5,7},{10,8},{11,9},{8,1... | collective-permute-start | bytes 2359304 | tf_op jit(solution)/shard_map/ppermute | solution.py:26
  39.8 2.0 %collective-permute-start.4 = (f32[128,1536]{1,0:T(8,128)S(1)}, f32[128,1536]{1,0:T(8,128)}, u32[]{:S(2)}, u32[]{:S(2)}) collective-permute-start(f32[128,1536]{1,0:T(8,128)S(1)} %pad_maximum_fusion.1), channel_id=1, source_target_pairs={{1,0},{2,1},{3,2},{0,3},{5,4},{6,5},{7,6},{4,7},{9,8},{10,9},{11,1... | collective-permute-start | bytes 2359304 | tf_op jit(solution)/shard_map/ppermute | solution.py:26
  41.8 1.2 fusion.14
  42.9 0.6 convolution_subtract_fusion.2
  44.2 26.7 %shard_map.31 = f32[128,128]{1,0:T(8,128)} custom-call(f32[128,128]{1,0:T(8,128)} %slice.132.a_ref), custom_call_target="tpu_custom_call" | custom-call | tf_op jit(solution)/shard_map/pallas_call | solution.py:63
  70.9 1.1 fusion.16
  73.1 26.7 %shard_map.32 = f32[128,128]{1,0:T(8,128)} custom-call(f32[128,128]{1,0:T(8,128)} %slice.136.a_ref), custom_call_target="tpu_custom_call" | custom-call | tf_op jit(solution)/shard_map/pallas_call | solution.py:63
  99.8 1.1 fusion.18
  100.9 0.9 convolution_subtract_fusion.4.a_ref
  101.8 26.7 %shard_map.33 = f32[128,128]{1,0:T(8,128)} custom-call(f32[128,128]{1,0:T(8,128)} %convolution_subtract_fusion.4.a_ref), custom_call_target="tpu_custom_call" | custom-call | tf_op jit(solution)/shard_map/pallas_call | solution.py:63
  128.5 1.6 fusion.27
  130.2 3.2 %maximum_subtract_fusion = f32[384,1536]{1,0:T(8,128)S(1)} fusion(f32[128,1536]{1,0:T(8,128)S(1)} %collective-permute-done.6, f32[128,1536]{1,0:T(8,128)S(1)} %collective-permute-done.5, f32[128,1536]{1,0:T(8,128)} %collective-permute-done.4, f32[384,128]{1,0:T(8,128)S(1)} %fusion.14, f32[128,1536]{1,0:T(8,128)S(1)} %fusion.27), kind=kOutput, calls=%fused_computation.6 | convolution fusion | flops 907739136 | bytes 5701632 | tf_op jit(solution)/shard_map/dot_general | solution.py:73
  133.4 0.8 fusion.10
  134.2 1.4 slice_subtract_fusion
  135.6 0.8 fusion.8
  136.4 0.8 convolution_subtract_fusion.1
  137.2 0.8 fusion.28
  138.2 2.4 %collective-permute-start.7 = (f32[512,1536]{1,0:T(8,128)S(1)}, f32[512,1536]{1,0:T(8,128)}, u32[]{:S(2)}, u32[]{:S(2)}) collective-permute-start(f32[512,1536]{1,0:T(8,128)S(1)} %pad_maximum_fusion), channel_id=1, source_target_pairs={{0,4},{4,0},{8,12},{12,8},{16,20},{20,16},{24,28},{28,24},{32,36},... | collective-permute-start | bytes 9437192 | tf_op jit(solution)/shard_map/ppermute | solution.py:18
  140.6 1.8 %fusion.23 = (f32[384,384]{1,0:T(8,128)S(1)}, f32[384,384]{1,0:T(8,128)S(1)}, f32[384,384]{1,0:T(8,128)S(1)}, f32[384,384]{1,0:T(8,128)S(1)}) fusion(f32[512,2048]{1,0:T(8,128)} %bitcast.32), kind=kLoop, calls=%fused_computation.47 | loop fusion | bytes 4718592 | tf_op jit(solution)/shard_map/slice | solution.py:145
  142.4 4.0 %convolution_subtract_fusion = f32[384,1536]{1,0:T(8,128)S(1)} fusion(f32[512,1536]{1,0:T(8,128)S(1)} %pad_maximum_fusion, f32[384,384]{1,0:T(8,128)S(1)} %get-tuple-element.7, f32[384,384]{1,0:T(8,128)S(1)} %get-tuple-element.8, f32[384,384]{1,0:T(8,128)S(1)} %get-tuple-element.9, f32[384,384]{1,0:T(8,128)S(1)} %get-tuple-element.6, s32[]{:T(128)S(6)} %select_n.35), kind=kOutput, calls=%fused_computation.2 | convolution fusion | flops 3626237952 | bytes 8650756 | tf_op jit(solution)/shard_map/dot_general | solution.py:148
  146.4 1.4 copy-done
  147.8 0.7 pad_maximum_fusion.3
  148.7 8.0 %collective-permute-done.8 = f32[128,512]{1,0:T(8,128)} collective-permute-done((f32[128,512]{1,0:T(8,128)}, f32[128,512]{1,0:T(8,128)}, u32[]{:S(2)}, u32[]{:S(2)}) %collective-permute-start.8) | collective-permute-done | bytes 262176 | tf_op jit(solution)/shard_map/ppermute | solution.py:18
  156.7 1.7 %add_bitcast_fusion = f32[1,128,512]{2,1,0:T(8,128)} fusion(f32[128,512]{1,0:T(8,128)} %collective-permute-done.8, f32[128,128]{1,0:T(8,128)S(1)} %get-tuple-element.11, f32[128,128]{1,0:T(8,128)S(1)} %get-tuple-element.12, f32[128,128]{1,0:T(8,128)S(1)} %get-tuple-element.13, f32[128,128]{1,0:T(8,128)S(1)} %get-tuple-element.10), kind=kLoop, calls=%fused_computation.36 | loop fusion | flops 262144 | bytes 786432 | tf_op jit(solution)/shard_map/broadcast_in_dim | solution.py:165
  158.3 6.1 %fusion = f32[1,384,1536]{2,1,0:T(8,128)S(1)} fusion(f32[512,1536]{1,0:T(8,128)} %collective-permute-done.7, f32[512,1536]{1,0:T(8,128)S(1)} %pad_maximum_fusion, s32[]{:T(128)S(6)} %select_n.35), kind=kOutput, calls=%fused_computation.4 | convolution fusion | flops 3624468480 | bytes 6291460 | tf_op jit(solution)/shard_map/dot_general | solution.py:156
  164.4 2.9 %maximum_select_fusion = f32[1,384,3072]{2,1,0:T(8,128)} fusion(f32[1,384,1536]{2,1,0:T(8,128)S(1)} %fusion, f32[1,384,1536]{2,1,0:T(8,128)S(1)} %bitcast.31, pred[]{:T(512)S(6)} %eq.5), kind=kLoop, calls=%fused_computation | loop fusion | flops 3538944 | bytes 9437185 | tf_op jit(solution)/shard_map/jit(_where)/select_n | solution.py:159
  (31 shorter events, 4.6 us)
Async XLA Ops:
  2.0 4.5 %collective-permute-start = (f32[128,512]{1,0:T(8,128)S(1)}, f32[128,512]{1,0:T(8,128)S(1)}, u32[]{:S(2)}, u32[]{:S(2)}) collective-permute-start(f32[128,512]{1,0:T(8,128)S(1)} %pad_maximum_fusion.2), channel_id=1, source_target_pairs={{0,4},{4,0},{8,12},{12,8},{16,20},{20,16},{24,28},{28,24},{32,36},... | collective-permute-start | bytes 786440 | tf_op jit(solution)/shard_map/ppermute | solution.py:18
  6.5 29.4 %collective-permute-start.1 = (f32[128,512]{1,0:T(8,128)S(1)}, f32[128,512]{1,0:T(8,128)S(1)}, u32[]{:S(2)}, u32[]{:S(2)}) collective-permute-start(f32[128,512]{1,0:T(8,128)S(1)} %fusion.22), channel_id=1, source_target_pairs={{1,0},{2,1},{3,2},{0,3},{5,4},{6,5},{7,6},{4,7},{9,8},{10,9},{11,1... | collective-permute-start | bytes 786440 | tf_op jit(solution)/shard_map/ppermute | solution.py:26
  7.3 28.6 %collective-permute-start.2 = (f32[128,512]{1,0:T(8,128)S(1)}, f32[128,512]{1,0:T(8,128)S(1)}, u32[]{:S(2)}, u32[]{:S(2)}) collective-permute-start(f32[128,512]{1,0:T(8,128)S(1)} %fusion.22), channel_id=1, source_target_pairs={{2,0},{3,1},{0,2},{1,3},{6,4},{7,5},{4,6},{5,7},{10,8},{11,9},{8,1... | collective-permute-start | bytes 786440 | tf_op jit(solution)/shard_map/ppermute | solution.py:26
  7.9 28.0 %collective-permute-start.3 = (f32[128,512]{1,0:T(8,128)S(1)}, f32[128,512]{1,0:T(8,128)S(1)}, u32[]{:S(2)}, u32[]{:S(2)}) collective-permute-start(f32[128,512]{1,0:T(8,128)S(1)} %fusion.22), channel_id=1, source_target_pairs={{3,0},{0,1},{1,2},{2,3},{7,4},{4,5},{5,6},{6,7},{11,8},{8,9},{9,10... | collective-permute-start | bytes 786440 | tf_op jit(solution)/shard_map/ppermute | solution.py:26
  36.5 93.6 %collective-permute-start.6 = (f32[128,1536]{1,0:T(8,128)S(1)}, f32[128,1536]{1,0:T(8,128)S(1)}, u32[]{:S(2)}, u32[]{:S(2)}) collective-permute-start(f32[128,1536]{1,0:T(8,128)S(1)} %pad_maximum_fusion.1), channel_id=1, source_target_pairs={{3,0},{0,1},{1,2},{2,3},{7,4},{4,5},{5,6},{6,7},{11,8},{8,9},{9,10... | collective-permute-start | bytes 2359304 | tf_op jit(solution)/shard_map/ppermute | solution.py:26
  38.1 92.1 %collective-permute-start.5 = (f32[128,1536]{1,0:T(8,128)S(1)}, f32[128,1536]{1,0:T(8,128)S(1)}, u32[]{:S(2)}, u32[]{:S(2)}) collective-permute-start(f32[128,1536]{1,0:T(8,128)S(1)} %pad_maximum_fusion.1), channel_id=1, source_target_pairs={{2,0},{3,1},{0,2},{1,3},{6,4},{7,5},{4,6},{5,7},{10,8},{11,9},{8,1... | collective-permute-start | bytes 2359304 | tf_op jit(solution)/shard_map/ppermute | solution.py:26
  39.8 90.3 %collective-permute-start.4 = (f32[128,1536]{1,0:T(8,128)S(1)}, f32[128,1536]{1,0:T(8,128)}, u32[]{:S(2)}, u32[]{:S(2)}) collective-permute-start(f32[128,1536]{1,0:T(8,128)S(1)} %pad_maximum_fusion.1), channel_id=1, source_target_pairs={{1,0},{2,1},{3,2},{0,3},{5,4},{6,5},{7,6},{4,7},{9,8},{10,9},{11,1... | collective-permute-start | bytes 2359304 | tf_op jit(solution)/shard_map/ppermute | solution.py:26
  130.1 3.2 %copy-start.2 = (f32[128,128]{1,0:T(8,128)S(1)}, f32[128,128]{1,0:T(8,128)}, u32[]{:S(2)}) copy-start(f32[128,128]{1,0:T(8,128)} %shard_map.31) | copy-start | bytes 196612
  134.2 1.5 copy-start.3
  135.6 1.6 copy-start.4
  138.2 20.1 %collective-permute-start.7 = (f32[512,1536]{1,0:T(8,128)S(1)}, f32[512,1536]{1,0:T(8,128)}, u32[]{:S(2)}, u32[]{:S(2)}) collective-permute-start(f32[512,1536]{1,0:T(8,128)S(1)} %pad_maximum_fusion), channel_id=1, source_target_pairs={{0,4},{4,0},{8,12},{12,8},{16,20},{20,16},{24,28},{28,24},{32,36},... | collective-permute-start | bytes 9437192 | tf_op jit(solution)/shard_map/ppermute | solution.py:18
  146.4 1.4 copy-start
  148.5 8.2 %collective-permute-start.8 = (f32[128,512]{1,0:T(8,128)}, f32[128,512]{1,0:T(8,128)}, u32[]{:S(2)}, u32[]{:S(2)}) collective-permute-start(f32[128,512]{1,0:T(8,128)} %pad_maximum_fusion.3), channel_id=1, source_target_pairs={{0,8},{4,12},{8,0},{12,4},{16,24},{20,28},{24,16},{28,20},{32,40},... | collective-permute-start | bytes 786440 | tf_op jit(solution)/shard_map/ppermute | solution.py:18
  158.3 6.1 %copy-start.1 = (f32[384,1536]{1,0:T(8,128)S(1)}, f32[384,1536]{1,0:T(8,128)}, u32[]{:S(2)}) copy-start(f32[384,1536]{1,0:T(8,128)} %copy-done) | copy-start | bytes 7077892

commit v4 on v3

--- a/solution.py
+++ b/solution.py
@@ -49,22 +49,23 @@
             x_row = w_ref[pl.ds(j, 1), :] * scale
             x_ref[pl.ds(j, 1), :] = x_row
             rows = s_ref[r0:, :]
-            col = jnp.transpose(jnp.broadcast_to(l_row, (n, n)))[r0:, :]
-            l_col = jnp.where(row_id > j, col, 0.0)
+            col = jnp.sum(jnp.where(lane == j, rows, 0.0), axis=1, keepdims=True)
+            l_col = jnp.where(row_id > j, col * scale, 0.0)
             s_ref[r0:, :] = rows - l_col * l_row
             w_ref[r0:, :] = w_ref[r0:, :] - l_col * x_row
             return carry
 
-        lax.fori_loop(0, 8, step, 0)
+        lax.fori_loop(0, 8, step, 0, unroll=4)
 
 
 def inverse_factor(a):
-    n = a.shape[0]
+    n = BLOCK
     return pl.pallas_call(
         _inv_factor_kernel,
         out_shape=jax.ShapeDtypeStruct((n, n), jnp.float32),
-        in_specs=[pl.BlockSpec(memory_space=pltpu.VMEM)],
-        out_specs=pl.BlockSpec(memory_space=pltpu.VMEM),
+        grid=(1,),
+        in_specs=[pl.BlockSpec((n, n), lambda i: (0, 0))],
+        out_specs=pl.BlockSpec((n, n), lambda i: (0, 0)),
         scratch_shapes=[pltpu.VMEM((n, n), jnp.float32), pltpu.VMEM((n, n), jnp.float32)],
     )(a)
 
@@ -86,7 +87,7 @@
     panels = []
     inverses = []
     for k in range(nb):
-        diag = first_diag if k == 0 else trailing[:BLOCK, :BLOCK]
+        diag = first_diag if k == 0 else trailing
         inv = inverse_factor(diag)
         inverses.append(inv)
         if k + 1 < nb:

time: 168 us -> 122 us (0.73)
  Pallas kernels: 107 us -> 59.7 us
  matrix products: 24.8 us -> 27 us
    pallas_call x4, Pallas kernels: 107 us -> 59.7 us  [inverse_factor(): pl.pallas_call(_inv_factor_kernel, out_shape=jax.ShapeDtypeStruct((n, n),...]
    dot_general x6, matrix products: 5.32 us -> 8.71 us  [mm_nt(): lax.dot_general(a, b, (((1,), (1,)), ((), ())), precision=HIGHEST, prefer...]
  transfers between devices with their start and end apart: 9 -> 9, of which waited for: 2 -> 2; matrix products, arithmetic and copies ran while one was open for 10% -> 16% of each run, Pallas kernels for 64% -> 49%
where the time goes in v4:
time: 122 us; the launch traced here: 121 us
  Pallas kernels  59.7 us (49%)
  matrix products  27 us (22%)
  starting transfers between devices  12.9 us (11%)
  waiting for transfers between devices  9.11 us (7%)
  other arithmetic  6.21 us (5%)
  local copies, waits for them, and re-layouts  5.26 us (4%)
    pallas_call x4, Pallas kernels, inverse_factor(): pl.pallas_call(_inv_factor_kernel, out_shape=jax.ShapeDtypeStruct((n, n),...  59.7 us
    ppermute x3, waiting for transfers between devices, partner(): return lax.ppermute(value, axis, pairs)  9.09 us
    dot_general x6, matrix products, mm_nt(): lax.dot_general(a, b, (((1,), (1,)), ((), ())), precision=HIGHEST, prefer...  8.71 us
    dot_general x7, matrix products, mm(): return jnp.dot(a, b, precision=HIGHEST, preferred_element_type=jnp.float32)  8.24 us
    ppermute x6, starting transfers between devices, gather_layer(): pieces.append(lax.ppermute(value, 'layer', pairs))  7.27 us
    dot_general x1, matrix products, condense(): lax.dot_general(factor_own, joined_sib, contract, precision=HIGHEST, pref...  6.07 us
    ppermute x3, starting transfers between devices, partner(): return lax.ppermute(value, axis, pairs)  5.58 us
    dot_general x1, matrix products, condense(): lax.dot_general(factor_own, joined_own, contract, precision=HIGHEST, pref...  3.99 us
  transfers between devices with their start and end apart: 9, of which 2 were waited for; matrix products, arithmetic and copies ran while one was open for 16% of the time, Pallas kernels for 49%

profile of v4, /device:TPU:1, one launch (start us, length us, event | category | flops | bytes accessed | tf_op | source)
XLA Modules:
  0.0 121.0 jit_solution(4918719221689789088)
XLA Ops:
  0.6 1.3 %slice_bitcast_fusion = f32[128,2048]{1,0:T(8,128)S(1)} fusion(f32[1,512,2048]{2,1,0:T(8,128)} %param.1), kind=kLoop, calls=%fused_computation.26 | loop fusion | bytes 2097152 | tf_op jit(solution)/shard_map/slice | solution.py:123
  2.0 3.3 %collective-permute-start = (f32[128,512]{1,0:T(8,128)S(1)}, f32[128,512]{1,0:T(8,128)S(1)}, u32[]{:S(2)}, u32[]{:S(2)}) collective-permute-start(f32[128,512]{1,0:T(8,128)S(1)} %pad_maximum_fusion.2), channel_id=1, source_target_pairs={{0,4},{4,0},{8,12},{12,8},{16,20},{20,16},{24,28},{28,24},{32,36},... | collective-permute-start | bytes 786440 | tf_op jit(solution)/shard_map/ppermute | solution.py:18
  5.4 1.1 collective-permute-done
  6.5 0.8 collective-permute-start.1
  9.2 14.9 %shard_map.30 = f32[128,128]{1,0:T(8,128)} custom-call(f32[128,128]{1,0:T(8,128)} %constant_dynamic-slice_fusion.a_ref), custom_call_target="tpu_custom_call" | custom-call | tf_op jit(solution)/shard_map/pallas_call | solution.py:63
  24.7 1.6 %collective-permute-start.6 = (f32[128,1536]{1,0:T(8,128)S(1)}, f32[128,1536]{1,0:T(8,128)S(1)}, u32[]{:S(2)}, u32[]{:S(2)}) collective-permute-start(f32[128,1536]{1,0:T(8,128)S(1)} %pad_maximum_fusion.1), channel_id=1, source_target_pairs={{3,0},{0,1},{1,2},{2,3},{7,4},{4,5},{5,6},{6,7},{11,8},{8,9},{9,10... | collective-permute-start | bytes 2359304 | tf_op jit(solution)/shard_map/ppermute | solution.py:26
  26.3 1.7 %collective-permute-start.5 = (f32[128,1536]{1,0:T(8,128)S(1)}, f32[128,1536]{1,0:T(8,128)S(1)}, u32[]{:S(2)}, u32[]{:S(2)}) collective-permute-start(f32[128,1536]{1,0:T(8,128)S(1)} %pad_maximum_fusion.1), channel_id=1, source_target_pairs={{2,0},{3,1},{0,2},{1,3},{6,4},{7,5},{4,6},{5,7},{10,8},{11,9},{8,1... | collective-permute-start | bytes 2359304 | tf_op jit(solution)/shard_map/ppermute | solution.py:26
  28.0 2.0 %collective-permute-start.4 = (f32[128,1536]{1,0:T(8,128)S(1)}, f32[128,1536]{1,0:T(8,128)S(1)}, u32[]{:S(2)}, u32[]{:S(2)}) collective-permute-start(f32[128,1536]{1,0:T(8,128)S(1)} %pad_maximum_fusion.1), channel_id=1, source_target_pairs={{1,0},{2,1},{3,2},{0,3},{5,4},{6,5},{7,6},{4,7},{9,8},{10,9},{11,1... | collective-permute-start | bytes 2359304 | tf_op jit(solution)/shard_map/ppermute | solution.py:26
  30.0 1.2 fusion.14
  31.2 1.5 %convolution_subtract_fusion.2.a_ref = f32[384,384]{1,0:T(8,128)} fusion(f32[384,128]{1,0:T(8,128)S(1)} %fusion.14, f32[512,512]{1,0:T(8,128)S(1)} %fusion.4), kind=kOutput, calls=%fused_computation.16 | convolution fusion | flops 226639872 | bytes 1572864 | tf_op jit(solution)/shard_map/dot_general | solution.py:78
  32.6 14.9 %shard_map.31 = f32[128,128]{1,0:T(8,128)} custom-call(f32[384,384]{1,0:T(8,128)} %convolution_subtract_fusion.2.a_ref), custom_call_target="tpu_custom_call" | custom-call | tf_op jit(solution)/shard_map/pallas_call | solution.py:63
  47.5 1.2 fusion.16
  48.7 2.0 %convolution_subtract_fusion.3.a_ref = f32[256,256]{1,0:T(8,128)} fusion(f32[256,128]{1,0:T(8,128)S(1)} %fusion.16, f32[384,384]{1,0:T(8,128)} %convolution_subtract_fusion.2.a_ref), kind=kOutput, calls=%fused_computation.17 | convolution fusion | flops 100728832 | bytes 786432 | tf_op jit(solution)/shard_map/dot_general | solution.py:78
  50.8 14.9 %shard_map.32 = f32[128,128]{1,0:T(8,128)} custom-call(f32[256,256]{1,0:T(8,128)} %convolution_subtract_fusion.3.a_ref), custom_call_target="tpu_custom_call" | custom-call | tf_op jit(solution)/shard_map/pallas_call | solution.py:63
  65.7 1.1 fusion.18
  66.8 1.7 %convolution_subtract_fusion.4.a_ref = f32[128,128]{1,0:T(8,128)} fusion(f32[128,128]{1,0:T(8,128)S(1)} %fusion.18, f32[256,256]{1,0:T(8,128)} %convolution_subtract_fusion.3.a_ref), kind=kOutput, calls=%fused_computation.18 | convolution fusion | flops 25182208 | bytes 262144 | tf_op jit(solution)/shard_map/dot_general | solution.py:78
  68.5 14.9 %shard_map.33 = f32[128,128]{1,0:T(8,128)} custom-call(f32[128,128]{1,0:T(8,128)} %convolution_subtract_fusion.4.a_ref), custom_call_target="tpu_custom_call" | custom-call | tf_op jit(solution)/shard_map/pallas_call | solution.py:63
  83.4 1.6 %fusion.27 = f32[128,1536]{1,0:T(8,128)S(1)} fusion(f32[128,128]{1,0:T(8,128)} %shard_map.30, f32[128,1536]{1,0:T(8,128)S(1)} %pad_maximum_fusion.1), kind=kOutput, calls=%fused_computation.51 | convolution fusion | flops 301989888 | bytes 1638400 | tf_op jit(solution)/shard_map/dot_general | solution.py:74
  85.1 2.1 %maximum_subtract_fusion = f32[384,1536]{1,0:T(8,128)S(1)} fusion(f32[128,1536]{1,0:T(8,128)S(1)} %collective-permute-done.6, f32[128,1536]{1,0:T(8,128)S(1)} %collective-permute-done.5, f32[128,1536]{1,0:T(8,128)S(1)} %collective-permute-done.4, f32[384,128]{1,0:T(8,128)S(1)} %fusion.14, f32[128,1536]{1,0:T(8,128)S(1)} %fusion.27), kind=kOutput, calls=%fused_computation.6 | convolution fusion | flops 907739136 | bytes 5701632 | tf_op jit(solution)/shard_map/dot_general | solution.py:74
  87.2 0.8 fusion.10
  88.0 1.4 %slice_subtract_fusion = f32[256,1536]{1,0:T(8,128)S(1)} fusion(f32[384,1536]{1,0:T(8,128)S(1)} %maximum_subtract_fusion, f32[256,128]{1,0:T(8,128)S(1)} %fusion.16, f32[128,1536]{1,0:T(8,128)S(1)} %fusion.10), kind=kOutput, calls=%fused_computation.15 | convolution fusion | flops 604372992 | bytes 4063232 | tf_op jit(solution)/shard_map/dot_general | solution.py:74
  89.5 0.8 fusion.8
  90.3 0.8 convolution_subtract_fusion.1
  91.1 0.8 fusion.28
  92.1 2.1 %collective-permute-start.7 = (f32[512,1536]{1,0:T(8,128)S(1)}, f32[512,1536]{1,0:T(8,128)}, u32[]{:S(2)}, u32[]{:S(2)}) collective-permute-start(f32[512,1536]{1,0:T(8,128)S(1)} %pad_maximum_fusion), channel_id=1, source_target_pairs={{0,4},{4,0},{8,12},{12,8},{16,20},{20,16},{24,28},{28,24},{32,36},... | collective-permute-start | bytes 9437192 | tf_op jit(solution)/shard_map/ppermute | solution.py:18
  94.2 1.8 %fusion.23 = (f32[384,384]{1,0:T(8,128)S(1)}, f32[384,384]{1,0:T(8,128)S(1)}, f32[384,384]{1,0:T(8,128)S(1)}, f32[384,384]{1,0:T(8,128)S(1)}) fusion(f32[512,2048]{1,0:T(8,128)} %bitcast.32), kind=kLoop, calls=%fused_computation.47 | loop fusion | bytes 4718592 | tf_op jit(solution)/shard_map/slice | solution.py:146
  96.0 4.0 %convolution_subtract_fusion = f32[384,1536]{1,0:T(8,128)S(1)} fusion(f32[512,1536]{1,0:T(8,128)S(1)} %pad_maximum_fusion, f32[384,384]{1,0:T(8,128)S(1)} %get-tuple-element.7, f32[384,384]{1,0:T(8,128)S(1)} %get-tuple-element.8, f32[384,384]{1,0:T(8,128)S(1)} %get-tuple-element.9, f32[384,384]{1,0:T(8,128)S(1)} %get-tuple-element.6, s32[]{:T(128)S(6)} %select_n.35), kind=kOutput, calls=%fused_computation.2 | convolution fusion | flops 3626237952 | bytes 8650756 | tf_op jit(solution)/shard_map/dot_general | solution.py:149
  100.0 1.4 %copy-done = f32[384,1536]{1,0:T(8,128)} copy-done((f32[384,1536]{1,0:T(8,128)}, f32[384,1536]{1,0:T(8,128)S(1)}, u32[]{:S(2)}) %copy-start) | copy-done | bytes 2359320
  102.3 8.0 %collective-permute-done.8 = f32[128,512]{1,0:T(8,128)} collective-permute-done((f32[128,512]{1,0:T(8,128)}, f32[128,512]{1,0:T(8,128)}, u32[]{:S(2)}, u32[]{:S(2)}) %collective-permute-start.8) | collective-permute-done | bytes 262176 | tf_op jit(solution)/shard_map/ppermute | solution.py:18
  110.3 1.7 %add_bitcast_fusion = f32[1,128,512]{2,1,0:T(8,128)} fusion(f32[128,512]{1,0:T(8,128)} %collective-permute-done.8, f32[128,128]{1,0:T(8,128)S(1)} %get-tuple-element.11, f32[128,128]{1,0:T(8,128)S(1)} %get-tuple-element.12, f32[128,128]{1,0:T(8,128)S(1)} %get-tuple-element.13, f32[128,128]{1,0:T(8,128)S(1)} %get-tuple-element.10), kind=kLoop, calls=%fused_computation.36 | loop fusion | flops 262144 | bytes 786432 | tf_op jit(solution)/shard_map/broadcast_in_dim | solution.py:166
  112.0 6.1 %fusion = f32[1,384,1536]{2,1,0:T(8,128)S(1)} fusion(f32[512,1536]{1,0:T(8,128)} %collective-permute-done.7, f32[512,1536]{1,0:T(8,128)S(1)} %pad_maximum_fusion, s32[]{:T(128)S(6)} %select_n.35), kind=kOutput, calls=%fused_computation.4 | convolution fusion | flops 3624468480 | bytes 6291460 | tf_op jit(solution)/shard_map/dot_general | solution.py:157
  118.1 2.9 %maximum_select_fusion = f32[1,384,3072]{2,1,0:T(8,128)} fusion(f32[1,384,1536]{2,1,0:T(8,128)S(1)} %fusion, f32[1,384,1536]{2,1,0:T(8,128)S(1)} %bitcast.31, pred[]{:T(512)S(6)} %eq.5), kind=kLoop, calls=%fused_computation | loop fusion | flops 3538944 | bytes 9437185 | tf_op jit(solution)/shard_map/jit(_where)/select_n | solution.py:160
  (29 shorter events, 3.7 us)
Async XLA Ops:
  2.0 4.5 %collective-permute-start = (f32[128,512]{1,0:T(8,128)S(1)}, f32[128,512]{1,0:T(8,128)S(1)}, u32[]{:S(2)}, u32[]{:S(2)}) collective-permute-start(f32[128,512]{1,0:T(8,128)S(1)} %pad_maximum_fusion.2), channel_id=1, source_target_pairs={{0,4},{4,0},{8,12},{12,8},{16,20},{20,16},{24,28},{28,24},{32,36},... | collective-permute-start | bytes 786440 | tf_op jit(solution)/shard_map/ppermute | solution.py:18
  6.5 17.6 %collective-permute-start.1 = (f32[128,512]{1,0:T(8,128)S(1)}, f32[128,512]{1,0:T(8,128)S(1)}, u32[]{:S(2)}, u32[]{:S(2)}) collective-permute-start(f32[128,512]{1,0:T(8,128)S(1)} %fusion.22), channel_id=1, source_target_pairs={{1,0},{2,1},{3,2},{0,3},{5,4},{6,5},{7,6},{4,7},{9,8},{10,9},{11,1... | collective-permute-start | bytes 786440 | tf_op jit(solution)/shard_map/ppermute | solution.py:26
  7.3 16.8 %collective-permute-start.2 = (f32[128,512]{1,0:T(8,128)S(1)}, f32[128,512]{1,0:T(8,128)S(1)}, u32[]{:S(2)}, u32[]{:S(2)}) collective-permute-start(f32[128,512]{1,0:T(8,128)S(1)} %fusion.22), channel_id=1, source_target_pairs={{2,0},{3,1},{0,2},{1,3},{6,4},{7,5},{4,6},{5,7},{10,8},{11,9},{8,1... | collective-permute-start | bytes 786440 | tf_op jit(solution)/shard_map/ppermute | solution.py:26
  7.9 16.3 %collective-permute-start.3 = (f32[128,512]{1,0:T(8,128)S(1)}, f32[128,512]{1,0:T(8,128)S(1)}, u32[]{:S(2)}, u32[]{:S(2)}) collective-permute-start(f32[128,512]{1,0:T(8,128)S(1)} %fusion.22), channel_id=1, source_target_pairs={{3,0},{0,1},{1,2},{2,3},{7,4},{4,5},{5,6},{6,7},{11,8},{8,9},{9,10... | collective-permute-start | bytes 786440 | tf_op jit(solution)/shard_map/ppermute | solution.py:26
  24.7 60.4 %collective-permute-start.6 = (f32[128,1536]{1,0:T(8,128)S(1)}, f32[128,1536]{1,0:T(8,128)S(1)}, u32[]{:S(2)}, u32[]{:S(2)}) collective-permute-start(f32[128,1536]{1,0:T(8,128)S(1)} %pad_maximum_fusion.1), channel_id=1, source_target_pairs={{3,0},{0,1},{1,2},{2,3},{7,4},{4,5},{5,6},{6,7},{11,8},{8,9},{9,10... | collective-permute-start | bytes 2359304 | tf_op jit(solution)/shard_map/ppermute | solution.py:26
  26.3 58.8 %collective-permute-start.5 = (f32[128,1536]{1,0:T(8,128)S(1)}, f32[128,1536]{1,0:T(8,128)S(1)}, u32[]{:S(2)}, u32[]{:S(2)}) collective-permute-start(f32[128,1536]{1,0:T(8,128)S(1)} %pad_maximum_fusion.1), channel_id=1, source_target_pairs={{2,0},{3,1},{0,2},{1,3},{6,4},{7,5},{4,6},{5,7},{10,8},{11,9},{8,1... | collective-permute-start | bytes 2359304 | tf_op jit(solution)/shard_map/ppermute | solution.py:26
  28.0 57.1 %collective-permute-start.4 = (f32[128,1536]{1,0:T(8,128)S(1)}, f32[128,1536]{1,0:T(8,128)S(1)}, u32[]{:S(2)}, u32[]{:S(2)}) collective-permute-start(f32[128,1536]{1,0:T(8,128)S(1)} %pad_maximum_fusion.1), channel_id=1, source_target_pairs={{1,0},{2,1},{3,2},{0,3},{5,4},{6,5},{7,6},{4,7},{9,8},{10,9},{11,1... | collective-permute-start | bytes 2359304 | tf_op jit(solution)/shard_map/ppermute | solution.py:26
  85.1 2.1 %copy-start.3 = (f32[128,128]{1,0:T(8,128)S(1)}, f32[128,128]{1,0:T(8,128)}, u32[]{:S(2)}) copy-start(f32[128,128]{1,0:T(8,128)} %shard_map.31) | copy-start | bytes 196612
  88.0 1.5 %copy-start.2 = (f32[128,128]{1,0:T(8,128)S(1)}, f32[128,128]{1,0:T(8,128)}, u32[]{:S(2)}) copy-start(f32[128,128]{1,0:T(8,128)} %shard_map.32) | copy-start | bytes 196612
  89.5 1.6 %copy-start.4 = (f32[128,128]{1,0:T(8,128)S(1)}, f32[128,128]{1,0:T(8,128)}, u32[]{:S(2)}) copy-start(f32[128,128]{1,0:T(8,128)} %shard_map.33) | copy-start | bytes 196612
  92.1 19.9 %collective-permute-start.7 = (f32[512,1536]{1,0:T(8,128)S(1)}, f32[512,1536]{1,0:T(8,128)}, u32[]{:S(2)}, u32[]{:S(2)}) collective-permute-start(f32[512,1536]{1,0:T(8,128)S(1)} %pad_maximum_fusion), channel_id=1, source_target_pairs={{0,4},{4,0},{8,12},{12,8},{16,20},{20,16},{24,28},{28,24},{32,36},... | collective-permute-start | bytes 9437192 | tf_op jit(solution)/shard_map/ppermute | solution.py:18
  100.0 1.4 %copy-start = (f32[384,1536]{1,0:T(8,128)}, f32[384,1536]{1,0:T(8,128)S(1)}, u32[]{:S(2)}) copy-start(f32[384,1536]{1,0:T(8,128)S(1)} %convolution_subtract_fusion) | copy-start | bytes 7077892
  102.1 8.2 %collective-permute-start.8 = (f32[128,512]{1,0:T(8,128)}, f32[128,512]{1,0:T(8,128)}, u32[]{:S(2)}, u32[]{:S(2)}) collective-permute-start(f32[128,512]{1,0:T(8,128)} %pad_maximum_fusion.3), channel_id=1, source_target_pairs={{0,8},{4,12},{8,0},{12,4},{16,24},{20,28},{24,16},{28,20},{32,40},... | collective-permute-start | bytes 786440 | tf_op jit(solution)/shard_map/ppermute | solution.py:18
  112.0 6.1 %copy-start.1 = (f32[384,1536]{1,0:T(8,128)S(1)}, f32[384,1536]{1,0:T(8,128)}, u32[]{:S(2)}) copy-start(f32[384,1536]{1,0:T(8,128)} %copy-done) | copy-start | bytes 7077892

commit v5 on v3

--- a/solution.py
+++ b/solution.py
@@ -44,18 +44,18 @@
             j = r0 + i
             row_j = s_ref[pl.ds(j, 1), :]
             d = jnp.sum(jnp.where(lane == j, row_j, 0.0), axis=1, keepdims=True)
-            scale = 1.0 / jnp.sqrt(d)
+            scale = lax.rsqrt(d)
             l_row = jnp.where(lane >= j, row_j * scale, 0.0)
             x_row = w_ref[pl.ds(j, 1), :] * scale
             x_ref[pl.ds(j, 1), :] = x_row
             rows = s_ref[r0:, :]
-            col = jnp.transpose(jnp.broadcast_to(l_row, (n, n)))[r0:, :]
-            l_col = jnp.where(row_id > j, col, 0.0)
+            col = jnp.sum(jnp.where(lane == j, rows, 0.0), axis=1, keepdims=True)
+            l_col = jnp.where(row_id > j, col * scale, 0.0)
             s_ref[r0:, :] = rows - l_col * l_row
             w_ref[r0:, :] = w_ref[r0:, :] - l_col * x_row
             return carry
 
-        lax.fori_loop(0, 8, step, 0)
+        lax.fori_loop(0, 8, step, 0, unroll=4)
 
 
 def inverse_factor(a):

time: 168 us -> 117 us (0.70)
  Pallas kernels: 107 us -> 55.7 us
    pallas_call x4, Pallas kernels: 107 us -> 55.7 us  [inverse_factor(): pl.pallas_call(_inv_factor_kernel, out_shape=jax.ShapeDtypeStruct((n, n),...]
  transfers between devices with their start and end apart: 9 -> 9, of which waited for: 2 -> 2; matrix products, arithmetic and copies ran while one was open for 10% -> 15% of each run, Pallas kernels for 64% -> 48%
where the time goes in v5:
time: 117 us; the launch traced here: 116 us
  Pallas kernels  55.7 us (48%)
  matrix products  24.8 us (21%)
  starting transfers between devices  12.9 us (11%)
  waiting for transfers between devices  9.1 us (8%)
  local copies, waits for them, and re-layouts  6.53 us (6%)
  other arithmetic  6.21 us (5%)
    pallas_call x4, Pallas kernels, inverse_factor(): pl.pallas_call(_inv_factor_kernel, out_shape=jax.ShapeDtypeStruct((n, n),...  55.7 us
    dot_general x7, matrix products, mm(): return jnp.dot(a, b, precision=HIGHEST, preferred_element_type=jnp.float32)  9.39 us
    ppermute x3, waiting for transfers between devices, partner(): return lax.ppermute(value, axis, pairs)  9.09 us
    ppermute x6, starting transfers between devices, gather_layer(): pieces.append(lax.ppermute(value, 'layer', pairs))  7.27 us
    dot_general x1, matrix products, condense(): lax.dot_general(factor_own, joined_sib, contract, precision=HIGHEST, pref...  6.07 us
    ppermute x3, starting transfers between devices, partner(): return lax.ppermute(value, axis, pairs)  5.58 us
    dot_general x6, matrix products, mm_nt(): lax.dot_general(a, b, (((1,), (1,)), ((), ())), precision=HIGHEST, prefer...  5.31 us
    dot_general x1, matrix products, condense(): lax.dot_general(factor_own, joined_own, contract, precision=HIGHEST, pref...  3.99 us
  transfers between devices with their start and end apart: 9, of which 2 were waited for; matrix products, arithmetic and copies ran while one was open for 15% of the time, Pallas kernels for 48%

profile of v5, /device:TPU:1, one launch (start us, length us, event | category | flops | bytes accessed | tf_op | source)
XLA Modules:
  0.0 116.0 jit_solution(7490478589999444507)
XLA Ops:
  0.6 1.3 %slice_bitcast_fusion = f32[128,2048]{1,0:T(8,128)S(1)} fusion(f32[1,512,2048]{2,1,0:T(8,128)} %param.1), kind=kLoop, calls=%fused_computation.26 | loop fusion | bytes 2097152 | tf_op jit(solution)/shard_map/slice | solution.py:122
  2.0 3.3 %collective-permute-start = (f32[128,512]{1,0:T(8,128)S(1)}, f32[128,512]{1,0:T(8,128)S(1)}, u32[]{:S(2)}, u32[]{:S(2)}) collective-permute-start(f32[128,512]{1,0:T(8,128)S(1)} %pad_maximum_fusion.2), channel_id=1, source_target_pairs={{0,4},{4,0},{8,12},{12,8},{16,20},{20,16},{24,28},{28,24},{32,36},... | collective-permute-start | bytes 786440 | tf_op jit(solution)/shard_map/ppermute | solution.py:18
  5.4 1.1 collective-permute-done
  6.5 0.8 collective-permute-start.1
  8.5 0.6 constant_dynamic-slice_fusion.a_ref
  9.2 13.9 %shard_map.30 = f32[128,128]{1,0:T(8,128)} custom-call(f32[128,128]{1,0:T(8,128)} %constant_dynamic-slice_fusion.a_ref), custom_call_target="tpu_custom_call" | custom-call | tf_op jit(solution)/shard_map/pallas_call | solution.py:63
  23.7 1.6 %collective-permute-start.6 = (f32[128,1536]{1,0:T(8,128)S(1)}, f32[128,1536]{1,0:T(8,128)S(1)}, u32[]{:S(2)}, u32[]{:S(2)}) collective-permute-start(f32[128,1536]{1,0:T(8,128)S(1)} %pad_maximum_fusion.1), channel_id=1, source_target_pairs={{3,0},{0,1},{1,2},{2,3},{7,4},{4,5},{5,6},{6,7},{11,8},{8,9},{9,10... | collective-permute-start | bytes 2359304 | tf_op jit(solution)/shard_map/ppermute | solution.py:26
  25.3 1.7 %collective-permute-start.5 = (f32[128,1536]{1,0:T(8,128)S(1)}, f32[128,1536]{1,0:T(8,128)S(1)}, u32[]{:S(2)}, u32[]{:S(2)}) collective-permute-start(f32[128,1536]{1,0:T(8,128)S(1)} %pad_maximum_fusion.1), channel_id=1, source_target_pairs={{2,0},{3,1},{0,2},{1,3},{6,4},{7,5},{4,6},{5,7},{10,8},{11,9},{8,1... | collective-permute-start | bytes 2359304 | tf_op jit(solution)/shard_map/ppermute | solution.py:26
  27.0 2.0 %collective-permute-start.4 = (f32[128,1536]{1,0:T(8,128)S(1)}, f32[128,1536]{1,0:T(8,128)}, u32[]{:S(2)}, u32[]{:S(2)}) collective-permute-start(f32[128,1536]{1,0:T(8,128)S(1)} %pad_maximum_fusion.1), channel_id=1, source_target_pairs={{1,0},{2,1},{3,2},{0,3},{5,4},{6,5},{7,6},{4,7},{9,8},{10,9},{11,1... | collective-permute-start | bytes 2359304 | tf_op jit(solution)/shard_map/ppermute | solution.py:26
  29.0 1.2 %fusion.14 = f32[384,128]{1,0:T(8,128)S(1)} fusion(f32[128,128]{1,0:T(8,128)} %shard_map.30, f32[512,512]{1,0:T(8,128)S(1)} %fusion.4), kind=kOutput, calls=%fused_computation.37 | convolution fusion | flops 75497472 | bytes 458752 | tf_op jit(solution)/shard_map/dot_general | solution.py:77
  31.4 13.9 %shard_map.31 = f32[128,128]{1,0:T(8,128)} custom-call(f32[128,128]{1,0:T(8,128)} %slice.132.a_ref), custom_call_target="tpu_custom_call" | custom-call | tf_op jit(solution)/shard_map/pallas_call | solution.py:63
  45.4 1.1 fusion.16
  47.5 13.9 %shard_map.32 = f32[128,128]{1,0:T(8,128)} custom-call(f32[128,128]{1,0:T(8,128)} %slice.136.a_ref), custom_call_target="tpu_custom_call" | custom-call | tf_op jit(solution)/shard_map/pallas_call | solution.py:63
  61.4 1.1 fusion.18
  62.5 0.9 convolution_subtract_fusion.4.a_ref
  63.4 13.9 %shard_map.33 = f32[128,128]{1,0:T(8,128)} custom-call(f32[128,128]{1,0:T(8,128)} %convolution_subtract_fusion.4.a_ref), custom_call_target="tpu_custom_call" | custom-call | tf_op jit(solution)/shard_map/pallas_call | solution.py:63
  77.3 1.6 %fusion.27 = f32[128,1536]{1,0:T(8,128)S(1)} fusion(f32[128,128]{1,0:T(8,128)} %shard_map.30, f32[128,1536]{1,0:T(8,128)S(1)} %pad_maximum_fusion.1), kind=kOutput, calls=%fused_computation.51 | convolution fusion | flops 301989888 | bytes 1638400 | tf_op jit(solution)/shard_map/dot_general | solution.py:73
  79.0 3.2 %maximum_subtract_fusion = f32[384,1536]{1,0:T(8,128)S(1)} fusion(f32[128,1536]{1,0:T(8,128)S(1)} %collective-permute-done.6, f32[128,1536]{1,0:T(8,128)S(1)} %collective-permute-done.5, f32[128,1536]{1,0:T(8,128)} %collective-permute-done.4, f32[384,128]{1,0:T(8,128)S(1)} %fusion.14, f32[128,1536]{1,0:T(8,128)S(1)} %fusion.27), kind=kOutput, calls=%fused_computation.6 | convolution fusion | flops 907739136 | bytes 5701632 | tf_op jit(solution)/shard_map/dot_general | solution.py:73
  82.2 0.8 fusion.10
  83.0 1.5 %slice_subtract_fusion = f32[256,1536]{1,0:T(8,128)S(1)} fusion(f32[384,1536]{1,0:T(8,128)S(1)} %maximum_subtract_fusion, f32[256,128]{1,0:T(8,128)S(1)} %fusion.16, f32[128,1536]{1,0:T(8,128)S(1)} %fusion.10), kind=kOutput, calls=%fused_computation.15 | convolution fusion | flops 604372992 | bytes 4063232 | tf_op jit(solution)/shard_map/dot_general | solution.py:73
  84.5 0.8 fusion.8
  85.3 0.8 convolution_subtract_fusion.1
  86.1 0.8 fusion.28
  87.1 2.1 %collective-permute-start.7 = (f32[512,1536]{1,0:T(8,128)S(1)}, f32[512,1536]{1,0:T(8,128)}, u32[]{:S(2)}, u32[]{:S(2)}) collective-permute-start(f32[512,1536]{1,0:T(8,128)S(1)} %pad_maximum_fusion), channel_id=1, source_target_pairs={{0,4},{4,0},{8,12},{12,8},{16,20},{20,16},{24,28},{28,24},{32,36},... | collective-permute-start | bytes 9437192 | tf_op jit(solution)/shard_map/ppermute | solution.py:18
  89.2 1.8 %fusion.23 = (f32[384,384]{1,0:T(8,128)S(1)}, f32[384,384]{1,0:T(8,128)S(1)}, f32[384,384]{1,0:T(8,128)S(1)}, f32[384,384]{1,0:T(8,128)S(1)}) fusion(f32[512,2048]{1,0:T(8,128)} %bitcast.32), kind=kLoop, calls=%fused_computation.47 | loop fusion | bytes 4718592 | tf_op jit(solution)/shard_map/slice | solution.py:145
  91.0 4.0 %convolution_subtract_fusion = f32[384,1536]{1,0:T(8,128)S(1)} fusion(f32[512,1536]{1,0:T(8,128)S(1)} %pad_maximum_fusion, f32[384,384]{1,0:T(8,128)S(1)} %get-tuple-element.7, f32[384,384]{1,0:T(8,128)S(1)} %get-tuple-element.8, f32[384,384]{1,0:T(8,128)S(1)} %get-tuple-element.9, f32[384,384]{1,0:T(8,128)S(1)} %get-tuple-element.6, s32[]{:T(128)S(6)} %select_n.35), kind=kOutput, calls=%fused_computation.2 | convolution fusion | flops 3626237952 | bytes 8650756 | tf_op jit(solution)/shard_map/dot_general | solution.py:148
  95.0 1.4 %copy-done = f32[384,1536]{1,0:T(8,128)} copy-done((f32[384,1536]{1,0:T(8,128)}, f32[384,1536]{1,0:T(8,128)S(1)}, u32[]{:S(2)}) %copy-start) | copy-done | bytes 2359320
  96.4 0.7 pad_maximum_fusion.3
  97.3 8.0 %collective-permute-done.8 = f32[128,512]{1,0:T(8,128)} collective-permute-done((f32[128,512]{1,0:T(8,128)}, f32[128,512]{1,0:T(8,128)}, u32[]{:S(2)}, u32[]{:S(2)}) %collective-permute-start.8) | collective-permute-done | bytes 262176 | tf_op jit(solution)/shard_map/ppermute | solution.py:18
  105.3 1.7 %add_bitcast_fusion = f32[1,128,512]{2,1,0:T(8,128)} fusion(f32[128,512]{1,0:T(8,128)} %collective-permute-done.8, f32[128,128]{1,0:T(8,128)S(1)} %get-tuple-element.11, f32[128,128]{1,0:T(8,128)S(1)} %get-tuple-element.12, f32[128,128]{1,0:T(8,128)S(1)} %get-tuple-element.13, f32[128,128]{1,0:T(8,128)S(1)} %get-tuple-element.10), kind=kLoop, calls=%fused_computation.36 | loop fusion | flops 262144 | bytes 786432 | tf_op jit(solution)/shard_map/broadcast_in_dim | solution.py:165
  107.0 6.1 %fusion = f32[1,384,1536]{2,1,0:T(8,128)S(1)} fusion(f32[512,1536]{1,0:T(8,128)} %collective-permute-done.7, f32[512,1536]{1,0:T(8,128)S(1)} %pad_maximum_fusion, s32[]{:T(128)S(6)} %select_n.35), kind=kOutput, calls=%fused_computation.4 | convolution fusion | flops 3624468480 | bytes 6291460 | tf_op jit(solution)/shard_map/dot_general | solution.py:156
  113.1 2.9 %maximum_select_fusion = f32[1,384,3072]{2,1,0:T(8,128)} fusion(f32[1,384,1536]{2,1,0:T(8,128)S(1)} %fusion, f32[1,384,1536]{2,1,0:T(8,128)S(1)} %bitcast.31, pred[]{:T(512)S(6)} %eq.5), kind=kLoop, calls=%fused_computation | loop fusion | flops 3538944 | bytes 9437185 | tf_op jit(solution)/shard_map/jit(_where)/select_n | solution.py:159
  (31 shorter events, 4.6 us)
Async XLA Ops:
  2.0 4.5 %collective-permute-start = (f32[128,512]{1,0:T(8,128)S(1)}, f32[128,512]{1,0:T(8,128)S(1)}, u32[]{:S(2)}, u32[]{:S(2)}) collective-permute-start(f32[128,512]{1,0:T(8,128)S(1)} %pad_maximum_fusion.2), channel_id=1, source_target_pairs={{0,4},{4,0},{8,12},{12,8},{16,20},{20,16},{24,28},{28,24},{32,36},... | collective-permute-start | bytes 786440 | tf_op jit(solution)/shard_map/ppermute | solution.py:18
  6.5 16.6 %collective-permute-start.1 = (f32[128,512]{1,0:T(8,128)S(1)}, f32[128,512]{1,0:T(8,128)S(1)}, u32[]{:S(2)}, u32[]{:S(2)}) collective-permute-start(f32[128,512]{1,0:T(8,128)S(1)} %fusion.22), channel_id=1, source_target_pairs={{1,0},{2,1},{3,2},{0,3},{5,4},{6,5},{7,6},{4,7},{9,8},{10,9},{11,1... | collective-permute-start | bytes 786440 | tf_op jit(solution)/shard_map/ppermute | solution.py:26
  7.3 15.8 %collective-permute-start.2 = (f32[128,512]{1,0:T(8,128)S(1)}, f32[128,512]{1,0:T(8,128)S(1)}, u32[]{:S(2)}, u32[]{:S(2)}) collective-permute-start(f32[128,512]{1,0:T(8,128)S(1)} %fusion.22), channel_id=1, source_target_pairs={{2,0},{3,1},{0,2},{1,3},{6,4},{7,5},{4,6},{5,7},{10,8},{11,9},{8,1... | collective-permute-start | bytes 786440 | tf_op jit(solution)/shard_map/ppermute | solution.py:26
  7.9 15.3 %collective-permute-start.3 = (f32[128,512]{1,0:T(8,128)S(1)}, f32[128,512]{1,0:T(8,128)S(1)}, u32[]{:S(2)}, u32[]{:S(2)}) collective-permute-start(f32[128,512]{1,0:T(8,128)S(1)} %fusion.22), channel_id=1, source_target_pairs={{3,0},{0,1},{1,2},{2,3},{7,4},{4,5},{5,6},{6,7},{11,8},{8,9},{9,10... | collective-permute-start | bytes 786440 | tf_op jit(solution)/shard_map/ppermute | solution.py:26
  23.7 55.3 %collective-permute-start.6 = (f32[128,1536]{1,0:T(8,128)S(1)}, f32[128,1536]{1,0:T(8,128)S(1)}, u32[]{:S(2)}, u32[]{:S(2)}) collective-permute-start(f32[128,1536]{1,0:T(8,128)S(1)} %pad_maximum_fusion.1), channel_id=1, source_target_pairs={{3,0},{0,1},{1,2},{2,3},{7,4},{4,5},{5,6},{6,7},{11,8},{8,9},{9,10... | collective-permute-start | bytes 2359304 | tf_op jit(solution)/shard_map/ppermute | solution.py:26
  25.3 53.7 %collective-permute-start.5 = (f32[128,1536]{1,0:T(8,128)S(1)}, f32[128,1536]{1,0:T(8,128)S(1)}, u32[]{:S(2)}, u32[]{:S(2)}) collective-permute-start(f32[128,1536]{1,0:T(8,128)S(1)} %pad_maximum_fusion.1), channel_id=1, source_target_pairs={{2,0},{3,1},{0,2},{1,3},{6,4},{7,5},{4,6},{5,7},{10,8},{11,9},{8,1... | collective-permute-start | bytes 2359304 | tf_op jit(solution)/shard_map/ppermute | solution.py:26
  27.0 52.0 %collective-permute-start.4 = (f32[128,1536]{1,0:T(8,128)S(1)}, f32[128,1536]{1,0:T(8,128)}, u32[]{:S(2)}, u32[]{:S(2)}) collective-permute-start(f32[128,1536]{1,0:T(8,128)S(1)} %pad_maximum_fusion.1), channel_id=1, source_target_pairs={{1,0},{2,1},{3,2},{0,3},{5,4},{6,5},{7,6},{4,7},{9,8},{10,9},{11,1... | collective-permute-start | bytes 2359304 | tf_op jit(solution)/shard_map/ppermute | solution.py:26
  79.0 3.3 %copy-start.2 = (f32[128,128]{1,0:T(8,128)S(1)}, f32[128,128]{1,0:T(8,128)}, u32[]{:S(2)}) copy-start(f32[128,128]{1,0:T(8,128)} %shard_map.31) | copy-start | bytes 196612
  83.0 1.5 %copy-start.3 = (f32[128,128]{1,0:T(8,128)S(1)}, f32[128,128]{1,0:T(8,128)}, u32[]{:S(2)}) copy-start(f32[128,128]{1,0:T(8,128)} %shard_map.32) | copy-start | bytes 196612
  84.5 1.6 %copy-start.4 = (f32[128,128]{1,0:T(8,128)S(1)}, f32[128,128]{1,0:T(8,128)}, u32[]{:S(2)}) copy-start(f32[128,128]{1,0:T(8,128)} %shard_map.33) | copy-start | bytes 196612
  87.1 19.9 %collective-permute-start.7 = (f32[512,1536]{1,0:T(8,128)S(1)}, f32[512,1536]{1,0:T(8,128)}, u32[]{:S(2)}, u32[]{:S(2)}) collective-permute-start(f32[512,1536]{1,0:T(8,128)S(1)} %pad_maximum_fusion), channel_id=1, source_target_pairs={{0,4},{4,0},{8,12},{12,8},{16,20},{20,16},{24,28},{28,24},{32,36},... | collective-permute-start | bytes 9437192 | tf_op jit(solution)/shard_map/ppermute | solution.py:18
  95.0 1.4 %copy-start = (f32[384,1536]{1,0:T(8,128)}, f32[384,1536]{1,0:T(8,128)S(1)}, u32[]{:S(2)}) copy-start(f32[384,1536]{1,0:T(8,128)S(1)} %convolution_subtract_fusion) | copy-start | bytes 7077892
  97.2 8.2 %collective-permute-start.8 = (f32[128,512]{1,0:T(8,128)}, f32[128,512]{1,0:T(8,128)}, u32[]{:S(2)}, u32[]{:S(2)}) collective-permute-start(f32[128,512]{1,0:T(8,128)} %pad_maximum_fusion.3), channel_id=1, source_target_pairs={{0,8},{4,12},{8,0},{12,4},{16,24},{20,28},{24,16},{28,20},{32,40},... | collective-permute-start | bytes 786440 | tf_op jit(solution)/shard_map/ppermute | solution.py:18
  107.0 6.1 %copy-start.1 = (f32[384,1536]{1,0:T(8,128)S(1)}, f32[384,1536]{1,0:T(8,128)}, u32[]{:S(2)}) copy-start(f32[384,1536]{1,0:T(8,128)} %copy-done) | copy-start | bytes 7077892
